TPU v7x, 32 devices: a whole 2x2x4 slice. The times are simulated.
32 devices in a mesh: kv: 8 (over y, x, core), head: 4 (over z).
Axes of the slice: x: 2, y: 2, z: 4, core: 2. Of those that a mesh axis runs over, the one named last changes fastest.
Arguments:
- tokens: bfloat16 [128, 5120], P(None, 'kv'), may hold values from -6 to 6
- q_weight: bfloat16 [5120, 8192], P('kv', 'head'), may hold values from -0.078125 to 0.078125
- key_matrix: bfloat16 [5120, 1024], P('kv', 'head'), may hold values from -0.078125 to 0.078125
- value_matrix: bfloat16 [5120, 1024], P('kv', 'head'), may hold values from -0.078125 to 0.078125
- q_gain: float32 [64, 128], P('head'), may hold values from 0.4 to 45, as said below
- key_norm_scale: float32 [8, 128], P('head'), may hold values from 0.4 to 1.8
- stored_cache_keys: bfloat16 [32, 8192, 8, 128], P(None, 'kv', 'head'), may hold values from -6 to 6
- stored_cache_values: bfloat16 [32, 8192, 8, 128], P(None, 'kv', 'head'), may hold values from -6 to 6
- lengths: int32 [32], replicated, may hold values from 8 to 8192, as said below
- positions: int32 [32, 4], replicated, may hold values from 8 to 8195, as said below
- o_weight: bfloat16 [8192, 5120], P('head', 'kv'), may hold values from -0.0625 to 0.0625
Outputs:
- layer_out: bfloat16 [128, 5120], P('head', 'kv')
Inputs may be any that keep to these rules, and one draw needn't show every extreme that they name: `lengths`: every length is 8 or more; one request in each draw has exactly 8192 live positions. positions[r, 0] = lengths[r], and each later draft's position equals the previous one's or exceeds it by one; the request with 8192 live positions has its drafts at consecutive positions. `q_gain`: positive scales.
All inputs are finite; a program needn't handle non-finite values.
Results may differ from a plain program's by a relative error of at most 0.015.
Values may be sent and summed in bfloat16 or wider, within the bound.
No kernel may reach another device: no remote copies, remote signals or barrier semaphores. Data moves between devices by JAX's collectives and lax.ppermute only.
A program may use at most 128 MiB of HBM per device.

v0:
```python
import math

import jax
import jax.numpy as jnp
from jax import lax
from jax.sharding import PartitionSpec as P

EPSILON = 1e-06
ROPE_BASE = 1000000.0
NEG = -1e30


def merged(part, axis, combine):
    gathered = jax.tree.map(lambda a: lax.all_gather(a, axis), part)

    def take(source):
        return jax.tree.map(lambda a: lax.dynamic_index_in_dim(a, source, 0, False), gathered)

    return lax.fori_loop(
        1, lax.axis_size(axis), lambda source, state: combine(state, take(source)), take(0)
    )


def norm_rotate(proj, gain, pos_rows):
    heads, head_dim = gain.shape
    count = proj.shape[0]
    vec = proj.reshape(count, heads, head_dim)
    vec = vec * lax.rsqrt(jnp.mean(vec * vec, axis=-1, keepdims=True) + EPSILON) * gain
    half = head_dim // 2
    freq = ROPE_BASE ** (-(jnp.arange(half, dtype=jnp.float32) * 2.0 / head_dim))
    angle = pos_rows.astype(jnp.float32)[:, None, None] * freq
    cosine = jnp.cos(angle)
    sine = jnp.sin(angle)
    first = vec[..., :half]
    second = vec[..., half:]
    out = jnp.concatenate([first * cosine - second * sine, second * cosine + first * sine], axis=-1)
    return out.reshape(count, heads * head_dim).astype(jnp.bfloat16)


def combine(left, right):
    peak = jnp.maximum(left[0], right[0])
    left_ratio = jnp.exp(left[0] - peak)
    right_ratio = jnp.exp(right[0] - peak)
    return (
        peak,
        left[1] * left_ratio + right[1] * right_ratio,
        left[2] * left_ratio[..., None] + right[2] * right_ratio[..., None],
    )


def on_device(
    tokens,
    q_weight,
    key_matrix,
    value_matrix,
    q_gain,
    key_norm_scale,
    stored_cache_keys,
    stored_cache_values,
    lengths,
    positions,
    o_weight,
):
    rows = tokens.shape[0]
    reqs, drafts = positions.shape
    pos_rows = positions.reshape(rows)
    q_part = jnp.dot(tokens, q_weight, preferred_element_type=jnp.float32)
    k_part = jnp.dot(tokens, key_matrix, preferred_element_type=jnp.float32)
    v_part = jnp.dot(tokens, value_matrix, preferred_element_type=jnp.float32)
    q_sum, k_sum, v_sum = lax.psum((q_part, k_part, v_part), "kv")
    query_rows = norm_rotate(q_sum, q_gain, pos_rows)
    incoming_keys = norm_rotate(k_sum, key_norm_scale, pos_rows)
    incoming_values = v_sum.astype(jnp.bfloat16)
    kv_local, head_dim = key_norm_scale.shape
    group_size = q_gain.shape[0] // kv_local
    query_blocks = query_rows.reshape(reqs, drafts, kv_local, group_size, head_dim)
    scale = 1.0 / math.sqrt(head_dim)
    local_len = stored_cache_keys.shape[1]
    width = min(512, local_len)
    count = local_len // width
    offset = lax.axis_index("kv") * local_len

    def absorb(carry, keys, values, live):
        top, total, acc = carry
        scores = (
            jnp.einsum("rjkgd,rtkd->rjkgt", query_blocks, keys, preferred_element_type=jnp.float32)
            * scale
        )
        mask = live[:, :, None, None, :]
        top_new = jnp.maximum(top, jnp.max(jnp.where(mask, scores, NEG), axis=-1))
        ratio = jnp.exp(top - top_new)
        weights = jnp.where(mask, jnp.exp(scores - top_new[..., None]), 0.0)
        total = total * ratio + jnp.sum(weights, axis=-1)
        acc = acc * ratio[..., None] + jnp.einsum(
            "rjkgt,rtkd->rjkgd",
            weights.astype(jnp.bfloat16),
            values,
            preferred_element_type=jnp.float32,
        )
        return (top_new, total, acc)

    def block_step(index, carry):
        start = index * width
        keys = lax.dynamic_slice_in_dim(stored_cache_keys, start, width, 1)
        values = lax.dynamic_slice_in_dim(stored_cache_values, start, width, 1)
        where_pos = offset + start + jnp.arange(width, dtype=jnp.int32)
        live = jnp.broadcast_to(
            (where_pos[None, :] < lengths[:, None])[:, None, :], (reqs, drafts, width)
        )
        return absorb(carry, keys, values, live)

    stat_shape = (reqs, drafts, kv_local, group_size)
    carry = (
        jnp.full(stat_shape, NEG, jnp.float32),
        jnp.zeros(stat_shape, jnp.float32),
        jnp.zeros(stat_shape + (head_dim,), jnp.float32),
    )
    carry = lax.fori_loop(0, count, block_step, carry)
    order = jnp.arange(drafts, dtype=jnp.int32)
    seen = (order[None, :] == order[:, None])[None] | (order[None, :] < order[:, None])[None] & (
        positions[:, None, :] < positions[:, :, None]
    )
    draft_live = seen & (lax.axis_index("kv") == 0)
    carry = absorb(
        carry,
        incoming_keys.reshape(reqs, drafts, kv_local, head_dim),
        incoming_values.reshape(reqs, drafts, kv_local, head_dim),
        draft_live,
    )
    heads_local = kv_local * group_size
    top, total, acc = merged(carry, "kv", combine)
    attended = (acc / total[..., None]).astype(jnp.bfloat16).reshape(rows, heads_local * head_dim)
    return lax.psum_scatter(
        jnp.dot(attended, o_weight, preferred_element_type=jnp.float32).astype(jnp.bfloat16),
        "head",
        scatter_dimension=0,
        tiled=True,
    )


def solution(mesh):
    placed = (
        P(None, "kv"),
        P("kv", "head"),
        P("kv", "head"),
        P("kv", "head"),
        P("head", None),
        P("head", None),
        P(None, "kv", "head", None),
        P(None, "kv", "head", None),
        P(),
        P(),
        P("head", "kv"),
    )
    return jax.shard_map(
        on_device, mesh=mesh, in_specs=placed, out_specs=P("head", "kv"), check_vma=False
    )
```

profile of v0, /device:TPU:0, one launch (start us, length us, event | category | flops | bytes accessed | tf_op | source)
XLA Modules:
  0.0 266.7 jit_solution(2379651380921661182)
XLA Ops:
  6.6 1.7 copy-done
  8.3 1.5 convolution_bitcast_fusion.1
  9.8 1.2 copy.114
  11.0 0.2 convolution_bitcast_fusion.2
  11.2 0.7 copy.136
  12.0 0.2 fusion.37
  12.2 27.2 %all-reduce.5 = bf16[128,256]{1,0:T(8,128)(2,1)S(1)} all-reduce(f32[128,256]{1,0:T(8,128)S(1)} %fusion.37), channel_id=1, replica_groups=mesh['kv'=8,'head'=4] {'kv'}, use_global_device_ids=true, to_apply=%region_10.11 | all-reduce | flops 32768 | bytes 196608 | tf_op jit(solution)/shard_map/psum | solution.py:70
  39.9 0.3 multiply_cosine_fusion
  40.2 32.2 %all-reduce.4.cloned.1.call-done = (f32[128,16,128]{2,1,0:T(8,128)}, f32[128,2,128]{2,0,1:T(8,128)}) async-done(((f32[128,16,128]{2,1,0:T(8,128)}, f32[128,2,128]{2,0,1:T(8,128)}), (f32[128,16,128]{2,1,0:T(8,128)}, f32[128,2,128]{2,0,1:T(8,128)})) %all-reduce.4.cloned.1.call-update) | async-done | bytes 1179664 | tf_op jit(solution)/shard_map/psum | solution.py:70
  72.4 1.6 multiply_reduce_fusion
  74.1 1.0 multiply_reduce_fusion.1
  75.2 1.6 multiply_multiply_fusion
  76.8 1.0 multiply_multiply_fusion.1
  77.8 0.5 subtract_convert_fusion
  78.4 0.3 pad_maximum_fusion
  78.8 65.1 %while.38 = (s32[]{:T(128)}, f32[32,4,2,8]{3,1,2,0:T(4,128)S(1)}, f32[32,4,2,8]{3,1,2,0:T(4,128)S(1)}, f32[32,4,2,8,128]{4,3,1,2,0:T(8,128)}, s32[]{:T(128)}, /*...) while((s32[]{:T(128)}, f32[32,4,2,8]{3,1,2,0:T(4,128)S(1)}, ...), condition=%wide.region_5.6_spmd.clone, body=%wide.region_2.5_spmd.clone.sunk | while | flops 549218816 | bytes 82514272 | solution.py:118
  78.8 14.3 %constant_dynamic-slice_fusion.3 = (bf16[32,512,2,128]{3,2,1,0:T(2,128)(2,1)}, bf16[32,512,2,128]{3,2,1,0:T(2,128)(2,1)}) fusion(bf16[32,1024,2,128]{3,2,1,0:T(2,128)(2,1)} %get-tuple-element.663, s32[]{:T(128)S(6)} %select_n.81, bf16[32,1024,2,128]{3,2,1,0:T(2,128)(2,1)} %get-tuple-element.661), kind=kLoop, calls=%fused_computation.32.clone.1 | loop fusion | bytes 33554436 | tf_op jit(solution)/shard_map/while/body/eval_jaxpr/dynamic_slice | solution.py:105
  93.2 8.2 %fusion.59 = (f32[32,4,2,8]{3,1,2,0:T(4,128)S(1)}, f32[32,2,512,4,8]{2,4,3,1,0:T(8,128)}) fusion(pred[32,512]{1,0:T(8,128)(4,1)S(1)} %broadcast_compare_fusion.2, bf16[32,4,2,8,128]{4,3,1,2,0:T(8,128)(2,1)S(1)} %get-tuple-element.662, bf16[32,512,2,128]{3,2,1,0:T(2,128)(2,1)} %get-tuple-element.623), kind=kOutput, calls=%fused_computation.14.clone.1 | convolution fusion | flops 271579136 | bytes 13131776 | tf_op jit(solution)/shard_map/while/body/eval_jaxpr/rjkgd,rtkd->rjkgt/dot_general | solution.py:86
  101.5 3.5 %fusion.60 = f32[32,4,2,8]{3,1,2,0:T(4,128)S(1)} fusion(f32[32,2,512,4,8]{2,4,3,1,0:T(8,128)} %get-tuple-element.625, f32[32,4,2,8]{3,1,2,0:T(4,128)S(1)} %select_maximum_fusion.2, pred[32,512]{1,0:T(8,128)(4,1)S(1)} %broadcast_compare_fusion.2), kind=kLoop, calls=%fused_computation.18.clone.1 | loop fusion | flops 4192256 | bytes 4227072 | tf_op jit(solution)/shard_map/while/body/eval_jaxpr/reduce_sum | solution.py:93
  105.0 0.2 fusion.61
  105.2 6.1 %fusion.62 = f32[32,4,2,8,128]{4,3,1,2,0:T(8,128)} fusion(f32[32,2,512,4,8]{2,4,3,1,0:T(8,128)S(1)} %copy-done.2, f32[32,4,2,8]{3,1,2,0:T(4,128)S(1)} %select_maximum_fusion.2, pred[32,512]{1,0:T(8,128)(4,1)S(1)} %broadcast_compare_fusion.2, bf16[32,512,2,128]{3,2,1,0:T(2,128)(2,1)} %get-tuple-element.627, ...), kind=kOutput, calls=%fused_computation.24.clone.1 | convolution fusion | flops 273416192 | bytes 14712833 | tf_op jit(solution)/shard_map/while/body/eval_jaxpr/rjkgt,rtkd->rjkgd/dot_general | solution.py:94
  111.3 14.3 %constant_dynamic-slice_fusion.3 = (bf16[32,512,2,128]{3,2,1,0:T(2,128)(2,1)}, bf16[32,512,2,128]{3,2,1,0:T(2,128)(2,1)}) fusion(bf16[32,1024,2,128]{3,2,1,0:T(2,128)(2,1)} %get-tuple-element.663, s32[]{:T(128)S(6)} %select_n.81, bf16[32,1024,2,128]{3,2,1,0:T(2,128)(2,1)} %get-tuple-element.661), kind=kLoop, calls=%fused_computation.32.clone.1 | loop fusion | bytes 33554436 | tf_op jit(solution)/shard_map/while/body/eval_jaxpr/dynamic_slice | solution.py:105
  125.7 8.2 %fusion.59 = (f32[32,4,2,8]{3,1,2,0:T(4,128)S(1)}, f32[32,2,512,4,8]{2,4,3,1,0:T(8,128)}) fusion(pred[32,512]{1,0:T(8,128)(4,1)S(1)} %broadcast_compare_fusion.2, bf16[32,4,2,8,128]{4,3,1,2,0:T(8,128)(2,1)S(1)} %get-tuple-element.662, bf16[32,512,2,128]{3,2,1,0:T(2,128)(2,1)} %get-tuple-element.623), kind=kOutput, calls=%fused_computation.14.clone.1 | convolution fusion | flops 271579136 | bytes 13131776 | tf_op jit(solution)/shard_map/while/body/eval_jaxpr/rjkgd,rtkd->rjkgt/dot_general | solution.py:86
  133.9 3.5 %fusion.60 = f32[32,4,2,8]{3,1,2,0:T(4,128)S(1)} fusion(f32[32,2,512,4,8]{2,4,3,1,0:T(8,128)} %get-tuple-element.625, f32[32,4,2,8]{3,1,2,0:T(4,128)S(1)} %select_maximum_fusion.2, pred[32,512]{1,0:T(8,128)(4,1)S(1)} %broadcast_compare_fusion.2), kind=kLoop, calls=%fused_computation.18.clone.1 | loop fusion | flops 4192256 | bytes 4227072 | tf_op jit(solution)/shard_map/while/body/eval_jaxpr/reduce_sum | solution.py:93
  137.5 0.2 fusion.61
  137.7 6.2 %fusion.62 = f32[32,4,2,8,128]{4,3,1,2,0:T(8,128)} fusion(f32[32,2,512,4,8]{2,4,3,1,0:T(8,128)S(1)} %copy-done.2, f32[32,4,2,8]{3,1,2,0:T(4,128)S(1)} %select_maximum_fusion.2, pred[32,512]{1,0:T(8,128)(4,1)S(1)} %broadcast_compare_fusion.2, bf16[32,512,2,128]{3,2,1,0:T(2,128)(2,1)} %get-tuple-element.627, ...), kind=kOutput, calls=%fused_computation.24.clone.1 | convolution fusion | flops 273416192 | bytes 14712833 | tf_op jit(solution)/shard_map/while/body/eval_jaxpr/rjkgt,rtkd->rjkgd/dot_general | solution.py:94
  144.0 2.4 select_reduce_fusion
  146.4 0.6 fusion.27
  147.1 0.8 fusion.24
  147.9 1.1 copy.97
  149.1 10.3 %all-gather.1 = f32[256,4,2,8]{3,1,2,0:T(4,128)S(1)} all-gather(f32[32,4,2,8]{3,1,2,0:T(4,128)S(1)} %bitcast.120), channel_id=3, replica_groups=mesh['kv'=8,'head'=4] {'kv'}, dimensions={0}, use_global_device_ids=true | all-gather | bytes 73728 | tf_op jit(solution)/shard_map/all_gather | solution.py:14
  159.5 0.3 copy.101
  159.9 15.7 %all-gather = f32[256,4,2,8]{3,1,2,0:T(4,128)S(1)} all-gather(f32[32,4,2,8]{3,1,2,0:T(4,128)S(1)} %max.20), channel_id=2, replica_groups=mesh['kv'=8,'head'=4] {'kv'}, dimensions={0}, use_global_device_ids=true | all-gather | bytes 73728 | tf_op jit(solution)/shard_map/all_gather | solution.py:14
  175.7 0.3 copy.100
  176.1 30.7 %all-gather.5.cloned.1.call-done = f32[256,4,2,8,128]{4,3,2,1,0:T(8,128)} async-done(((f32[32,4,2,8,128]{4,3,2,1,0:T(8,128)}), f32[256,4,2,8,128]{4,3,2,1,0:T(8,128)}) %all-gather.5.cloned.1.call-update) | async-done | bytes 8388624 | tf_op jit(solution)/shard_map/all_gather | solution.py:14
  206.8 2.4 slice.28
  209.2 24.6 %while.37 = (s32[]{:T(128)}, f32[32,4,2,8]{0,3,2,1:T(8,128)S(1)}, f32[32,4,2,8]{0,3,2,1:T(8,128)S(1)}, f32[32,4,2,8,128]{4,3,2,1,0:T(8,128)}, f32[8,32,4,2,8]{1,...) while((s32[]{:T(128)}, f32[32,4,2,8]{0,3,2,1:T(8,128)S(1)}, ...), condition=%wide.region_12.13_spmd, body=%wide.region_11.12_spmd.sunk | while | flops 798725 | bytes 3260567 | solution.py:19
  209.5 3.2 %fusion.56 = f32[32,4,2,8,128]{4,3,2,1,0:T(8,128)} fusion(f32[8,32,4,2,8,128]{5,4,3,2,1,0:T(8,128)} %get-tuple-element.694, s32[]{:T(128)S(6)} %select_n.77, f32[32,4,2,8,128]{4,3,2,1,0:T(8,128)} %get-tuple-element.681, f32[32,4,2,8]{3,2,1,0:T(2,128)S(1)} %copy.141, f32[32,4,2,8]{3,2,1,0:T(2,128)S(1)} %copy.142), kind=kLoop, calls=%fused_computation.1.clone.1 | loop fusion | flops 786432 | bytes 3162116 | tf_op jit(solution)/shard_map/while/body/eval_jaxpr/add | solution.py:47
  213.0 3.2 %fusion.56 = f32[32,4,2,8,128]{4,3,2,1,0:T(8,128)} fusion(f32[8,32,4,2,8,128]{5,4,3,2,1,0:T(8,128)} %get-tuple-element.694, s32[]{:T(128)S(6)} %select_n.77, f32[32,4,2,8,128]{4,3,2,1,0:T(8,128)} %get-tuple-element.681, f32[32,4,2,8]{3,2,1,0:T(2,128)S(1)} %copy.141, f32[32,4,2,8]{3,2,1,0:T(2,128)S(1)} %copy.142), kind=kLoop, calls=%fused_computation.1.clone.1 | loop fusion | flops 786432 | bytes 3162116 | tf_op jit(solution)/shard_map/while/body/eval_jaxpr/add | solution.py:47
  216.5 3.2 %fusion.56 = f32[32,4,2,8,128]{4,3,2,1,0:T(8,128)} fusion(f32[8,32,4,2,8,128]{5,4,3,2,1,0:T(8,128)} %get-tuple-element.694, s32[]{:T(128)S(6)} %select_n.77, f32[32,4,2,8,128]{4,3,2,1,0:T(8,128)} %get-tuple-element.681, f32[32,4,2,8]{3,2,1,0:T(2,128)S(1)} %copy.141, f32[32,4,2,8]{3,2,1,0:T(2,128)S(1)} %copy.142), kind=kLoop, calls=%fused_computation.1.clone.1 | loop fusion | flops 786432 | bytes 3162116 | tf_op jit(solution)/shard_map/while/body/eval_jaxpr/add | solution.py:47
  220.1 3.2 %fusion.56 = f32[32,4,2,8,128]{4,3,2,1,0:T(8,128)} fusion(f32[8,32,4,2,8,128]{5,4,3,2,1,0:T(8,128)} %get-tuple-element.694, s32[]{:T(128)S(6)} %select_n.77, f32[32,4,2,8,128]{4,3,2,1,0:T(8,128)} %get-tuple-element.681, f32[32,4,2,8]{3,2,1,0:T(2,128)S(1)} %copy.141, f32[32,4,2,8]{3,2,1,0:T(2,128)S(1)} %copy.142), kind=kLoop, calls=%fused_computation.1.clone.1 | loop fusion | flops 786432 | bytes 3162116 | tf_op jit(solution)/shard_map/while/body/eval_jaxpr/add | solution.py:47
  223.6 3.2 %fusion.56 = f32[32,4,2,8,128]{4,3,2,1,0:T(8,128)} fusion(f32[8,32,4,2,8,128]{5,4,3,2,1,0:T(8,128)} %get-tuple-element.694, s32[]{:T(128)S(6)} %select_n.77, f32[32,4,2,8,128]{4,3,2,1,0:T(8,128)} %get-tuple-element.681, f32[32,4,2,8]{3,2,1,0:T(2,128)S(1)} %copy.141, f32[32,4,2,8]{3,2,1,0:T(2,128)S(1)} %copy.142), kind=kLoop, calls=%fused_computation.1.clone.1 | loop fusion | flops 786432 | bytes 3162116 | tf_op jit(solution)/shard_map/while/body/eval_jaxpr/add | solution.py:47
  227.1 3.2 %fusion.56 = f32[32,4,2,8,128]{4,3,2,1,0:T(8,128)} fusion(f32[8,32,4,2,8,128]{5,4,3,2,1,0:T(8,128)} %get-tuple-element.694, s32[]{:T(128)S(6)} %select_n.77, f32[32,4,2,8,128]{4,3,2,1,0:T(8,128)} %get-tuple-element.681, f32[32,4,2,8]{3,2,1,0:T(2,128)S(1)} %copy.141, f32[32,4,2,8]{3,2,1,0:T(2,128)S(1)} %copy.142), kind=kLoop, calls=%fused_computation.1.clone.1 | loop fusion | flops 786432 | bytes 3162116 | tf_op jit(solution)/shard_map/while/body/eval_jaxpr/add | solution.py:47
  230.6 3.2 %fusion.56 = f32[32,4,2,8,128]{4,3,2,1,0:T(8,128)} fusion(f32[8,32,4,2,8,128]{5,4,3,2,1,0:T(8,128)} %get-tuple-element.694, s32[]{:T(128)S(6)} %select_n.77, f32[32,4,2,8,128]{4,3,2,1,0:T(8,128)} %get-tuple-element.681, f32[32,4,2,8]{3,2,1,0:T(2,128)S(1)} %copy.141, f32[32,4,2,8]{3,2,1,0:T(2,128)S(1)} %copy.142), kind=kLoop, calls=%fused_computation.1.clone.1 | loop fusion | flops 786432 | bytes 3162116 | tf_op jit(solution)/shard_map/while/body/eval_jaxpr/add | solution.py:47
  233.9 2.5 divide_convert_fusion
  236.5 1.3 reshape.154
  237.7 3.0 %convolution_convert_fusion = bf16[128,640]{1,0:T(8,128)(2,1)} fusion(bf16[128,2048]{1,0:T(8,128)(2,1)S(1)} %reshape.154, bf16[2048,640]{1,0:T(8,128)(2,1)} %param.25), kind=kOutput, calls=%fused_computation.41 | convolution fusion | flops 335626240 | bytes 3309568 | tf_op jit(solution)/shard_map/dot_general | solution.py:134
  240.7 19.4 %reduce-scatter.2.cloned.1.call-done = bf16[32,640]{1,0:T(8,128)(2,1)} async-done(((bf16[128,640]{1,0:T(8,128)(2,1)}), bf16[32,640]{1,0:T(8,128)(2,1)}) %reduce-scatter.2.cloned.1.call-update) | async-done | bytes 40976 | tf_op jit(solution)/shard_map/reduce_scatter | solution.py:133
  (83 shorter events, 4.0 us)
Async XLA Ops:
  6.5 1.7 copy-start
  6.5 4.5 %copy-start.3 = (bf16[128,640]{1,0:T(8,128)(2,1)S(1)}, bf16[128,640]{1,0:T(8,128)(2,1)}, u32[]{:S(2)}) copy-start(bf16[128,640]{1,0:T(8,128)(2,1)} %param.15) | copy-start | bytes 491524
  6.5 4.5 %copy-start.4 = (bf16[640,256]{1,0:T(8,128)(2,1)S(1)}, bf16[640,256]{1,0:T(8,128)(2,1)}, u32[]{:S(2)}) copy-start(bf16[640,256]{1,0:T(8,128)(2,1)} %param.17) | copy-start | bytes 983044
  6.5 5.4 %copy-start.5 = (bf16[640,256]{1,0:T(8,128)(2,1)S(1)}, bf16[640,256]{1,0:T(8,128)(2,1)}, u32[]{:S(2)}) copy-start(bf16[640,256]{1,0:T(8,128)(2,1)} %param.18) | copy-start | bytes 983044
  6.5 32.8 %copy-start.8 = (s32[32,4]{0,1:T(4,128)S(1)}, s32[32,4]{0,1:T(4,128)}, u32[]{:S(2)}) copy-start(s32[32,4]{0,1:T(4,128)} %param.24) | copy-start | bytes 1540
  6.5 65.8 %all-reduce.4.cloned.1.call-start = ((), (), s32[]{:S(2)}) async-start(), calls=%async_computation.3 | async-start | bytes 2359296 | tf_op jit(solution)/shard_map/psum | solution.py:70
  9.8 65.4 %copy-start.7 = (f32[16,128]{1,0:T(8,128)S(1)}, f32[16,128]{1,0:T(8,128)}, u32[]{:S(2)}) copy-start(f32[16,128]{1,0:T(8,128)} %param.19) | copy-start | bytes 24580
  9.8 67.0 %copy-start.9 = (f32[2,128]{1,0:T(2,128)S(1)}, f32[2,128]{1,0:T(2,128)}, u32[]{:S(2)}) copy-start(f32[2,128]{1,0:T(2,128)} %param.20) | copy-start | bytes 3076
  11.9 194.9 %all-gather.5.cloned.1.call-start = ((), (), s32[]{:S(2)}) async-start(), calls=%async_computation.2 | async-start | bytes 9437184 | tf_op jit(solution)/shard_map/all_gather | solution.py:14
  75.2 3.6 %copy-start.6 = (s32[32]{0:T(128)S(1)}, s32[32]{0:T(128)}, u32[]{:S(2)}) copy-start(s32[32]{0:T(128)} %param.23) | copy-start | bytes 388
  101.4 3.8 %copy-start.2 = (f32[32,2,512,4,8]{2,4,3,1,0:T(8,128)S(1)}, f32[32,2,512,4,8]{2,4,3,1,0:T(8,128)}, u32[]{:S(2)}) copy-start(f32[32,2,512,4,8]{2,4,3,1,0:T(8,128)} %get-tuple-element.625) | copy-start | bytes 12582916 | tf_op jit(solution)/shard_map/while
  133.9 3.8 %copy-start.2 = (f32[32,2,512,4,8]{2,4,3,1,0:T(8,128)S(1)}, f32[32,2,512,4,8]{2,4,3,1,0:T(8,128)}, u32[]{:S(2)}) copy-start(f32[32,2,512,4,8]{2,4,3,1,0:T(8,128)} %get-tuple-element.625) | copy-start | bytes 12582916 | tf_op jit(solution)/shard_map/while
  143.9 3.2 %copy-start.10 = (f32[32,4,2,8,128]{4,3,1,2,0:T(8,128)S(1)}, f32[32,4,2,8,128]{4,3,1,2,0:T(8,128)}, u32[]{:S(2)}) copy-start(f32[32,4,2,8,128]{4,3,1,2,0:T(8,128)} %get-tuple-element.340) | copy-start | bytes 3145732
  149.1 111.1 %reduce-scatter.2.cloned.1.call-start = ((), (), s32[]{:S(2)}) async-start(), calls=%async_computation.1 | async-start | bytes 204800 | tf_op jit(solution)/shard_map/reduce_scatter | solution.py:133
  233.8 26.4 %copy-start.1 = (bf16[640,2048]{1,0:T(8,128)(2,1)S(1)}, bf16[640,2048]{1,0:T(8,128)(2,1)}, u32[]{:S(2)}) copy-start(bf16[640,2048]{1,0:T(8,128)(2,1)} %param.16) | copy-start | bytes 7864324
Sparse Core Ops, SparseCore 0:
  12.0 60.2 all-reduce.3
  149.2 57.5 all-gather.4
  240.9 19.2 reduce-scatter.1
where the time goes:
time: 267 us
  waiting for transfers between devices  82.4 us (31%)
  blocking collectives  53.2 us (20%)
  local copies, waits for them, and re-layouts  40.5 us (15%)
  other arithmetic  40 us (15%)
  matrix products  36.8 us (14%)
  between operations  13.4 us (5%)
    psum x1, waiting for transfers between devices, on_device(): q_sum, k_sum, v_sum = lax.psum((q_part, k_part, v_part), 'kv')  32.2 us
    all_gather x1, waiting for transfers between devices, merged(): gathered = jax.tree.map(lambda a: lax.all_gather(a, axis), part)  30.7 us
    dynamic_slice x2, local copies, waits for them, and re-layouts, block_step(): values = lax.dynamic_slice_in_dim(stored_cache_values, start, width, 1)  28.6 us
    psum x1, blocking collectives, on_device(): q_sum, k_sum, v_sum = lax.psum((q_part, k_part, v_part), 'kv')  27.2 us
    all_gather x2, blocking collectives, merged(): gathered = jax.tree.map(lambda a: lax.all_gather(a, axis), part)  26 us
    add x7, other arithmetic, combine(): left[2] * left_ratio[..., None] + right[2] * right_ratio[..., None]  22.4 us
    reduce_scatter x1, waiting for transfers between devices, on_device(): lax.psum_scatter(jnp.dot(attended, o_weight, preferred_element_type=jnp.f...  19.4 us
    dot_general x3, matrix products, absorb(): jnp.einsum('rjkgd,rtkd->rjkgt', query_blocks, keys, preferred_element_typ...  18.8 us
  transfers between devices with their start and end apart: 3, of which 3 were waited for; matrix products, arithmetic and copies ran while one was open for 1% of the time, Pallas kernels for 0%

commit v1 on v0

v1 whole, which is shorter than its diff:
```python
import functools
import math

import jax
import jax.numpy as jnp
from jax import lax
from jax.experimental import pallas as pl
from jax.experimental.pallas import tpu as pltpu
from jax.sharding import PartitionSpec as P

EPSILON = 1e-06
ROPE_BASE = 1000000.0
NEG = -1e30


def norm_rotate(proj, gain, pos_rows):
    heads, head_dim = gain.shape
    count = proj.shape[0]
    vec = proj.reshape(count, heads, head_dim)
    vec = vec * lax.rsqrt(jnp.mean(vec * vec, axis=-1, keepdims=True) + EPSILON) * gain
    half = head_dim // 2
    freq = ROPE_BASE ** (-(jnp.arange(half, dtype=jnp.float32) * 2.0 / head_dim))
    angle = pos_rows.astype(jnp.float32)[:, None, None] * freq
    cosine = jnp.cos(angle)
    sine = jnp.sin(angle)
    first = vec[..., :half]
    second = vec[..., half:]
    out = jnp.concatenate([first * cosine - second * sine, second * cosine + first * sine], axis=-1)
    return out.reshape(count, heads * head_dim).astype(jnp.bfloat16)


def log2_exact(value):
    shift = value.bit_length() - 1
    assert (1 << shift) == value
    return shift


def cache_kernel(kreq, kblk, live, q_ref, k_ref, v_ref, acc_out, m_out, l_out, m_sc, l_sc, acc_sc,
                 *, nb, tb, kv_shift, g_shift, scale):
    step = pl.program_id(0)
    req = step // nb
    blk = step % nb

    @pl.when(blk == 0)
    def _():
        m_sc[...] = jnp.full(m_sc.shape, NEG, jnp.float32)
        l_sc[...] = jnp.zeros(l_sc.shape, jnp.float32)
        acc_sc[...] = jnp.zeros(acc_sc.shape, jnp.float32)

    count = live[req]
    start = blk * tb

    @pl.when(start < count)
    def _():
        q = q_ref[0]
        keys = k_ref[0]
        s = lax.dot_general(q, keys, (((1,), (1,)), ((), ())), preferred_element_type=jnp.float32)
        s = s * scale
        col = lax.broadcasted_iota(jnp.int32, s.shape, 1)
        row = lax.broadcasted_iota(jnp.int32, s.shape, 0)
        kv_mask = (1 << kv_shift) - 1
        valid = ((col >> kv_shift) + start < count) & (
            (col & kv_mask) == ((row >> g_shift) & kv_mask)
        )
        s = jnp.where(valid, s, NEG)
        m_prev = m_sc[...]
        m_new = jnp.maximum(m_prev, jnp.max(s, axis=1, keepdims=True))
        alpha = jnp.exp(m_prev - m_new)
        p = jnp.exp(s - m_new)
        l_sc[...] = alpha * l_sc[...] + jnp.sum(p, axis=1, keepdims=True)
        acc_sc[...] = alpha * acc_sc[...] + jnp.dot(
            p.astype(jnp.bfloat16), v_ref[0], preferred_element_type=jnp.float32
        )
        m_sc[...] = m_new

    @pl.when(blk == nb - 1)
    def _():
        acc_out[0] = acc_sc[...]
        m_out[0] = m_sc[...]
        l_out[0] = l_sc[...]


def cache_attention(q_blocks, keys, values, live, kv_local, group_size):
    reqs, rows, head_dim = q_blocks.shape
    flat_len = keys.shape[1]
    local_len = flat_len // kv_local
    tb = min(512, local_len)
    nb = local_len // tb
    steps = reqs * nb
    step_ids = jnp.arange(steps, dtype=jnp.int32)
    step_live = (step_ids % nb) * tb < live[step_ids // nb]
    last_live = lax.cummax(jnp.where(step_live, step_ids, 0), axis=0)
    kreq = last_live // nb
    kblk = last_live % nb
    kernel = functools.partial(
        cache_kernel,
        nb=nb,
        tb=tb,
        kv_shift=log2_exact(kv_local),
        g_shift=log2_exact(group_size),
        scale=1.0 / math.sqrt(head_dim),
    )
    kv_block = tb * kv_local
    grid_spec = pltpu.PrefetchScalarGridSpec(
        num_scalar_prefetch=3,
        grid=(steps,),
        in_specs=[
            pl.BlockSpec((1, rows, head_dim), lambda i, kr, kb, lv: (i // nb, 0, 0)),
            pl.BlockSpec((1, kv_block, head_dim), lambda i, kr, kb, lv: (kr[i], kb[i], 0)),
            pl.BlockSpec((1, kv_block, head_dim), lambda i, kr, kb, lv: (kr[i], kb[i], 0)),
        ],
        out_specs=[
            pl.BlockSpec((1, rows, head_dim), lambda i, kr, kb, lv: (i // nb, 0, 0)),
            pl.BlockSpec((1, rows, 1), lambda i, kr, kb, lv: (i // nb, 0, 0)),
            pl.BlockSpec((1, rows, 1), lambda i, kr, kb, lv: (i // nb, 0, 0)),
        ],
        scratch_shapes=[
            pltpu.VMEM((rows, 1), jnp.float32),
            pltpu.VMEM((rows, 1), jnp.float32),
            pltpu.VMEM((rows, head_dim), jnp.float32),
        ],
    )
    return pl.pallas_call(
        kernel,
        grid_spec=grid_spec,
        out_shape=[
            jax.ShapeDtypeStruct((reqs, rows, head_dim), jnp.float32),
            jax.ShapeDtypeStruct((reqs, rows, 1), jnp.float32),
            jax.ShapeDtypeStruct((reqs, rows, 1), jnp.float32),
        ],
        compiler_params=pltpu.CompilerParams(dimension_semantics=("arbitrary",)),
    )(kreq, kblk, live, q_blocks, keys, values)


def on_device(
    tokens,
    q_weight,
    key_matrix,
    value_matrix,
    q_gain,
    key_norm_scale,
    stored_cache_keys,
    stored_cache_values,
    lengths,
    positions,
    o_weight,
):
    rows = tokens.shape[0]
    reqs, drafts = positions.shape
    kv_size = lax.axis_size("kv")
    kv_idx = lax.axis_index("kv")
    own_rows = rows // kv_size
    own_reqs = own_rows // drafts
    row0 = kv_idx * own_rows
    kv_local, head_dim = key_norm_scale.shape
    heads_local = q_gain.shape[0]
    group_size = heads_local // kv_local

    q_part = jnp.dot(tokens, q_weight, preferred_element_type=jnp.float32)
    k_part = jnp.dot(tokens, key_matrix, preferred_element_type=jnp.float32)
    v_part = jnp.dot(tokens, value_matrix, preferred_element_type=jnp.float32)
    q_own, k_own, v_own = lax.psum_scatter(
        (q_part, k_part, v_part), "kv", scatter_dimension=0, tiled=True
    )
    pos_own = lax.dynamic_slice_in_dim(positions.reshape(rows), row0, own_rows)
    q_own = norm_rotate(q_own, q_gain, pos_own)
    k_own = norm_rotate(k_own, key_norm_scale, pos_own)
    v_own = v_own.astype(jnp.bfloat16)
    query_rows = lax.all_gather(q_own, "kv", axis=0, tiled=True)

    local_len = stored_cache_keys.shape[1]
    offset = kv_idx * local_len
    live = jnp.clip(lengths - offset, 0, local_len).astype(jnp.int32)
    q_blocks = query_rows.reshape(reqs, drafts * heads_local, head_dim)
    keys = stored_cache_keys.reshape(reqs, local_len * kv_local, head_dim)
    values = stored_cache_values.reshape(reqs, local_len * kv_local, head_dim)
    acc_c, m_c, l_c = cache_attention(q_blocks, keys, values, live, kv_local, group_size)
    acc_c = acc_c.reshape(rows, heads_local, head_dim)
    m_c = m_c.reshape(rows, heads_local)
    l_c = l_c.reshape(rows, heads_local)

    scale = 1.0 / math.sqrt(head_dim)
    q_d = q_own.reshape(own_reqs, drafts, kv_local, group_size, head_dim)
    k_d = k_own.reshape(own_reqs, drafts, kv_local, head_dim)
    v_d = v_own.reshape(own_reqs, drafts, kv_local, head_dim)
    s_d = jnp.einsum("rjkgd,rikd->rjkgi", q_d, k_d, preferred_element_type=jnp.float32) * scale
    pos_req = lax.dynamic_slice_in_dim(positions, kv_idx * own_reqs, own_reqs)
    order = jnp.arange(drafts, dtype=jnp.int32)
    seen = (order[None, :] == order[:, None])[None] | (order[None, :] < order[:, None])[None] & (
        pos_req[:, None, :] < pos_req[:, :, None]
    )
    mask_d = seen[:, :, None, None, :]
    s_d = jnp.where(mask_d, s_d, NEG)
    m_d = jnp.max(s_d, axis=-1)
    p_d = jnp.where(mask_d, jnp.exp(s_d - m_d[..., None]), 0.0)
    l_d = jnp.sum(p_d, axis=-1).reshape(own_rows, heads_local)
    acc_d = jnp.einsum(
        "rjkgi,rikd->rjkgd", p_d.astype(jnp.bfloat16), v_d, preferred_element_type=jnp.float32
    ).reshape(own_rows, heads_local, head_dim)
    m_d = m_d.reshape(own_rows, heads_local)

    m_mine = jnp.maximum(lax.dynamic_slice_in_dim(m_c, row0, own_rows), m_d)
    m_all = lax.dynamic_update_slice_in_dim(m_c, m_mine, row0, 0)
    top = lax.pmax(m_all, "kv")
    ratio = jnp.exp(m_c - top)
    acc_s, l_s = lax.psum_scatter(
        (acc_c * ratio[..., None], l_c * ratio), "kv", scatter_dimension=0, tiled=True
    )
    top_own = lax.dynamic_slice_in_dim(top, row0, own_rows)
    ratio_d = jnp.exp(m_d - top_own)
    acc_s = acc_s + acc_d * ratio_d[..., None]
    l_s = l_s + l_d * ratio_d
    attended = (acc_s / l_s[..., None]).astype(jnp.bfloat16).reshape(own_rows, heads_local * head_dim)
    attended = lax.all_gather(attended, "kv", axis=0, tiled=True)
    return lax.psum_scatter(
        jnp.dot(attended, o_weight, preferred_element_type=jnp.float32).astype(jnp.bfloat16),
        "head",
        scatter_dimension=0,
        tiled=True,
    )


def solution(mesh):
    placed = (
        P(None, "kv"),
        P("kv", "head"),
        P("kv", "head"),
        P("kv", "head"),
        P("head", None),
        P("head", None),
        P(None, "kv", "head", None),
        P(None, "kv", "head", None),
        P(),
        P(),
        P("head", "kv"),
    )
    return jax.shard_map(
        on_device, mesh=mesh, in_specs=placed, out_specs=P("head", "kv"), check_vma=False
    )
```

time: 267 us -> 296 us (1.11); the launches traced: 267 us -> 293 us
  waiting for transfers between devices: 82.4 us -> 156 us
  Pallas kernels: 0 us -> 55.2 us
  local copies, waits for them, and re-layouts: 40.5 us -> 4.45 us
  other arithmetic: 40 us -> 11.5 us
  matrix products: 36.8 us -> 9.19 us
  blocking collectives: 53.2 us -> 42.3 us
    reduce_scatter x0 -> x5, waiting for transfers between devices: none -> 137 us  [the longest x3 69.4 us: on_device(): lax.psum_scatter((q_part, k_part, v_part), 'kv', scatter_dimension=0, til...]
    pallas_call x0 -> x1, Pallas kernels: none -> 55.2 us  [cache_attention(): pl.pallas_call(kernel, grid_spec=grid_spec, out_shape=[jax.ShapeDtypeStru...]
    psum x1 -> x0, waiting for transfers between devices: 32.2 us -> none  [on_device(): q_sum, k_sum, v_sum = lax.psum((q_part, k_part, v_part), 'kv')]
    dot_general x6 -> x2, matrix products: 31.9 us -> 0.7 us  [the longest x1 0.42 us: on_device(): jnp.einsum('rjkgd,rikd->rjkgi', q_d, k_d, preferred_element_type=jnp.floa...]
    dynamic_slice x5 -> x2, local copies, waits for them, and re-layouts: 31 us -> 0.17 us  [on_device(): pos_req = lax.dynamic_slice_in_dim(positions, kv_idx * own_reqs, own_reqs)]
    all_gather x1 -> x0, waiting for transfers between devices: 30.7 us -> none  [merged(): gathered = jax.tree.map(lambda a: lax.all_gather(a, axis), part)]
    psum x1 -> x0, blocking collectives: 27.2 us -> none  [on_device(): q_sum, k_sum, v_sum = lax.psum((q_part, k_part, v_part), 'kv')]
    pmax x0 -> x1, blocking collectives: none -> 22.7 us  [on_device(): top = lax.pmax(m_all, 'kv')]
  transfers between devices with their start and end apart: 3 -> 6, of which waited for: 3 -> 5; matrix products, arithmetic and copies ran while one was open for 1% -> 6% of each run, Pallas kernels for 0% -> 19%
where the time goes in v1:
time: 296 us; the launch traced here: 293 us
  waiting for transfers between devices  156 us (53%)
  Pallas kernels  55.2 us (19%)
  blocking collectives  42.3 us (14%)
  between operations  13.8 us (5%)
  other arithmetic  11.5 us (4%)
  matrix products  9.19 us (3%)
  local copies, waits for them, and re-layouts  4.45 us (2%)
    reduce_scatter x3, waiting for transfers between devices, on_device(): lax.psum_scatter((q_part, k_part, v_part), 'kv', scatter_dimension=0, til...  69.4 us
    reduce_scatter x2, waiting for transfers between devices, on_device(): lax.psum_scatter((acc_c * ratio[..., None], l_c * ratio), 'kv', scatter_d...  67.2 us
    pallas_call x1, Pallas kernels, cache_attention(): pl.pallas_call(kernel, grid_spec=grid_spec, out_shape=[jax.ShapeDtypeStru...  55.2 us
    pmax x1, blocking collectives, on_device(): top = lax.pmax(m_all, 'kv')  22.7 us
    reduce_scatter x1, waiting for transfers between devices, on_device(): lax.psum_scatter(jnp.dot(attended, o_weight, preferred_element_type=jnp.f...  19.4 us
    all_gather x1, blocking collectives, on_device(): attended = lax.all_gather(attended, 'kv', axis=0, tiled=True)  9.79 us
    all_gather x1, blocking collectives, on_device(): query_rows = lax.all_gather(q_own, 'kv', axis=0, tiled=True)  9.77 us
  transfers between devices with their start and end apart: 6, of which 5 were waited for; matrix products, arithmetic and copies ran while one was open for 6% of the time, Pallas kernels for 19%

profile of v1, /device:TPU:0, one launch (start us, length us, event | category | flops | bytes accessed | tf_op | source)
XLA Modules:
  0.0 292.7 jit_solution(9195288263844967998)
XLA Ops:
  6.5 2.1 fusion.18
  8.7 2.6 fusion.17
  11.4 0.9 fusion.19
  12.5 0.8 gather_fusion
  13.2 0.1 copy.51
  13.3 0.1 reduce-window.9
  13.4 0.1 reduce
  13.5 0.5 and_select_fusion
  14.1 0.1 copy.52
  14.2 0.1 reshape.259
  14.4 0.1 copy.53
  14.5 0.1 dynamic-slice_convert_fusion
  14.5 0.1 multiply_cosine_fusion
  14.7 0.1 and_or_fusion
  14.7 31.7 %reduce-scatter.9.cloned.1.call-done = f32[16,256]{1,0:T(8,128)} async-done(((f32[128,256]{1,0:T(8,128)}), f32[16,256]{1,0:T(8,128)}) %reduce-scatter.9.cloned.1.call-update) | async-done | bytes 16400 | tf_op jit(solution)/shard_map/reduce_scatter | solution.py:162
  46.4 0.7 reshape.265
  47.2 0.1 multiply_reduce_fusion.1
  47.3 0.1 copy.55
  47.4 0.8 fusion.9
  48.2 0.1 subtract_convert_fusion
  48.2 0.1 pad_maximum_fusion
  48.3 37.7 %reduce-scatter.7.cloned.1.call-done = f32[16,2048]{1,0:T(8,128)} async-done(((f32[128,2048]{1,0:T(8,128)}), f32[16,2048]{1,0:T(8,128)}) %reduce-scatter.7.cloned.1.call-update) | async-done | bytes 131088 | tf_op jit(solution)/shard_map/reduce_scatter | solution.py:162
  86.0 0.9 copy.70
  87.0 0.1 multiply_reduce_fusion
  87.1 0.1 multiply_multiply_fusion
  87.2 0.1 multiply_subtract_fusion
  87.3 0.1 maximum_convert_fusion
  87.4 9.8 %all_gather.6 = bf16[128,2048]{1,0:T(8,128)(2,1)S(1)} all-gather(bf16[16,2048]{1,0:T(8,128)(2,1)S(1)} %bitcast.53), channel_id=1, replica_groups=mesh['kv'=8,'head'=4] {'kv'}, dimensions={0}, use_global_device_ids=true | all-gather | bytes 589824 | tf_op jit(solution)/shard_map/all_gather | solution.py:169
  97.2 1.0 reshape.260.q_ref
  98.2 55.2 %shard_map.109 = (f32[32,64,128]{2,1,0:T(8,128)}, f32[32,64,1]{2,1,0:T(8,128)}, f32[32,64,1]{2,1,0:T(8,128)}) custom-call(s32[64]{0:T(128)} %get-tuple-element.22.kreq, s32[64]{0:T(128)} %get-tuple-element.21.kblk, s32[32]{0:T(128)} %copy-done.1, bf16[32,64,128]{2,1,0:T(8,128)(2,1)} %reshape.260.q_ref, bf16[32,2048,128]{2,1,0:T(8,128)(2,1)} %bitcast.45, ...), custom_call_target="tpu_custom_call" | custom-call | tf_op jit(solution)/shard_map/pallas_call | solution.py:123
  153.4 1.6 reduce.2
  155.1 1.6 reduce.1
  156.7 0.4 fusion.16
  157.2 0.1 reshape.266
  157.3 22.7 %pmax.7 = f32[128,16]{1,0:T(8,128)S(1)} all-reduce(f32[128,16]{1,0:T(8,128)S(1)} %maximum_dynamic-update-slice_fusion), channel_id=1, replica_groups=mesh['kv'=8,'head'=4] {'kv'}, use_global_device_ids=true, to_apply=%region_6.7 | all-reduce | flops 2048 | bytes 16384 | tf_op jit(solution)/shard_map/pmax | solution.py:204
  180.0 0.6 fusion.15
  180.7 2.6 broadcast_multiply_fusion
  183.4 0.7 convert_element_type.36
  184.1 0.3 convolution_bitcast_fusion
  184.4 0.1 fusion.3
  184.6 0.1 reshape.270
  184.7 28.5 %reduce-scatter.15.cloned.1.call-done = f32[16,16]{1,0:T(8,128)} async-done(((f32[128,16]{1,0:T(8,128)}), f32[16,16]{1,0:T(8,128)}) %reduce-scatter.15.cloned.1.call-update) | async-done | bytes 1040 | tf_op jit(solution)/shard_map/reduce_scatter | solution.py:206
  213.1 0.7 multiply_add_fusion.1
  213.8 38.7 %reduce-scatter.11.cloned.1.call-done = f32[16,16,128]{2,1,0:T(8,128)} async-done(((f32[128,16,128]{2,1,0:T(8,128)}), f32[16,16,128]{2,1,0:T(8,128)}) %reduce-scatter.11.cloned.1.call-update) | async-done | bytes 131088 | tf_op jit(solution)/shard_map/reduce_scatter | solution.py:206
  252.5 1.0 divide_convert_fusion
  253.6 9.8 %all_gather.7 = bf16[128,2048]{1,0:T(8,128)(2,1)S(1)} all-gather(bf16[16,2048]{1,0:T(8,128)(2,1)S(1)} %bitcast.52), channel_id=1, replica_groups=mesh['kv'=8,'head'=4] {'kv'}, dimensions={0}, use_global_device_ids=true | all-gather | bytes 589824 | tf_op jit(solution)/shard_map/all_gather | solution.py:214
  263.4 3.0 %convolution_convert_fusion = bf16[128,640]{1,0:T(8,128)(2,1)} fusion(bf16[128,2048]{1,0:T(8,128)(2,1)S(1)} %all_gather.7, bf16[2048,640]{1,0:T(8,128)(2,1)} %param.21), kind=kOutput, calls=%fused_computation.1 | convolution fusion | flops 335626240 | bytes 3309568 | tf_op jit(solution)/shard_map/dot_general | solution.py:216
  266.4 19.4 %reduce-scatter.17.cloned.1.call-done = bf16[32,640]{1,0:T(8,128)(2,1)} async-done(((bf16[128,640]{1,0:T(8,128)(2,1)}), bf16[32,640]{1,0:T(8,128)(2,1)}) %reduce-scatter.17.cloned.1.call-update) | async-done | bytes 40976 | tf_op jit(solution)/shard_map/reduce_scatter | solution.py:215
  (48 shorter events, 0.8 us)
Async XLA Ops:
  6.5 2.2 copy-start
  6.5 39.9 %reduce-scatter.9.cloned.1.call-start = ((), (), s32[]{:S(2)}) async-start(), calls=%async_computation.7 | async-start | bytes 147456 | tf_op jit(solution)/shard_map/reduce_scatter | solution.py:162
  8.6 2.8 copy-start.2
  8.6 2.8 copy-start.3
  8.6 3.8 %copy-start.7 = (s32[32]{0:T(128)S(1)}, s32[32]{0:T(128)}, u32[]{:S(2)}) copy-start(s32[32]{0:T(128)} %param.19) | copy-start | bytes 388
  8.7 5.4 %copy-start.5 = (s32[32,4]{0,1:T(4,128)S(1)}, s32[32,4]{0,1:T(4,128)}, u32[]{:S(2)}) copy-start(s32[32,4]{0,1:T(4,128)} %param.20) | copy-start | bytes 1540
  8.7 38.7 %copy-start.6 = (f32[2,128]{1,0:T(2,128)S(1)}, f32[2,128]{1,0:T(2,128)}, u32[]{:S(2)}) copy-start(f32[2,128]{1,0:T(2,128)} %param.16) | copy-start | bytes 3076
  8.7 78.4 %copy-start.4 = (f32[16,128]{1,0:T(8,128)S(1)}, f32[16,128]{1,0:T(8,128)}, u32[]{:S(2)}) copy-start(f32[16,128]{1,0:T(8,128)} %param.15) | copy-start | bytes 24580
  8.7 77.3 %reduce-scatter.7.cloned.1.call-start = ((), (), s32[]{:S(2)}) async-start(), calls=%async_computation.6 | async-start | bytes 1179648 | tf_op jit(solution)/shard_map/reduce_scatter | solution.py:162
  11.4 172.0 %reduce-scatter.13.cloned.1.call-start = ((), (), s32[]{:S(2)}) async-start(), calls=%async_computation.9 | async-start | bytes 147456 | tf_op jit(solution)/shard_map/reduce_scatter | solution.py:162
  12.3 200.8 %reduce-scatter.15.cloned.1.call-start = ((), (), s32[]{:S(2)}) async-start(), calls=%async_computation.10 | async-start | bytes 73728 | tf_op jit(solution)/shard_map/reduce_scatter | solution.py:206
  12.4 85.8 %copy-start.1 = (s32[32]{0:T(128)}, s32[32]{0:T(128)S(1)}, u32[]{:S(2)}) copy-start(s32[32]{0:T(128)S(1)} %subtract_clamp_fusion.live) | copy-start | bytes 388
  180.7 71.9 %reduce-scatter.11.cloned.1.call-start = ((), (), s32[]{:S(2)}) async-start(), calls=%async_computation.8 | async-start | bytes 1179648 | tf_op jit(solution)/shard_map/reduce_scatter | solution.py:206
  183.3 102.5 %reduce-scatter.17.cloned.1.call-start = ((), (), s32[]{:S(2)}) async-start(), calls=%async_computation.11 | async-start | bytes 204800 | tf_op jit(solution)/shard_map/reduce_scatter | solution.py:215
Sparse Core Ops, SparseCore 0:
  10.4 36.0 reduce-scatter.8
  49.9 36.0 reduce-scatter.6
  89.3 33.3 reduce-scatter.12
  180.8 32.3 reduce-scatter.14
  216.5 36.0 reduce-scatter.10
  266.5 19.2 reduce-scatter.16

commit v2 on v1

v2 whole, which is shorter than its diff:
```python
import functools
import math

import jax
import jax.numpy as jnp
from jax import lax
from jax.experimental import pallas as pl
from jax.experimental.pallas import tpu as pltpu
from jax.sharding import PartitionSpec as P

EPSILON = 1e-06
ROPE_BASE = 1000000.0
NEG = -1e30


def norm_rotate(proj, gain, pos_rows):
    heads, head_dim = gain.shape
    count = proj.shape[0]
    vec = proj.reshape(count, heads, head_dim)
    vec = vec * lax.rsqrt(jnp.mean(vec * vec, axis=-1, keepdims=True) + EPSILON) * gain
    half = head_dim // 2
    freq = ROPE_BASE ** (-(jnp.arange(half, dtype=jnp.float32) * 2.0 / head_dim))
    angle = pos_rows.astype(jnp.float32)[:, None, None] * freq
    cosine = jnp.cos(angle)
    sine = jnp.sin(angle)
    first = vec[..., :half]
    second = vec[..., half:]
    out = jnp.concatenate([first * cosine - second * sine, second * cosine + first * sine], axis=-1)
    return out.reshape(count, heads * head_dim).astype(jnp.bfloat16)


def log2_exact(value):
    shift = value.bit_length() - 1
    assert (1 << shift) == value
    return shift


def cache_kernel(kgrp, live, q_ref, k_ref, v_ref, acc_out, m_out, l_out,
                 *, rb, chunk, kv_shift, g_shift, scale):
    step = pl.program_id(0)
    rows = q_ref.shape[1]
    width = chunk << kv_shift
    kv_mask = (1 << kv_shift) - 1
    col = lax.broadcasted_iota(jnp.int32, (rows, width), 1)
    row = lax.broadcasted_iota(jnp.int32, (rows, width), 0)
    same_head = (col & kv_mask) == ((row >> g_shift) & kv_mask)
    col_pos = col >> kv_shift
    for slot in range(rb):
        count = live[step * rb + slot]
        q = q_ref[slot]

        def body(c, carry):
            m_prev, l_prev, acc_prev = carry
            base = pl.multiple_of(c * width, width)
            keys = k_ref[slot, pl.ds(base, width), :]
            s = lax.dot_general(q, keys, (((1,), (1,)), ((), ())), preferred_element_type=jnp.float32)
            s = s * scale
            valid = same_head & (col_pos + c * chunk < count)
            s = jnp.where(valid, s, NEG)
            m_new = jnp.maximum(m_prev, jnp.max(s, axis=1, keepdims=True))
            alpha = jnp.exp(m_prev - m_new)
            p = jnp.exp(s - m_new)
            l_new = alpha * l_prev + jnp.sum(p, axis=1, keepdims=True)
            acc_new = alpha * acc_prev + jnp.dot(
                p.astype(jnp.bfloat16), v_ref[slot, pl.ds(base, width), :],
                preferred_element_type=jnp.float32,
            )
            return m_new, l_new, acc_new

        init = (
            jnp.full((rows, 1), NEG, jnp.float32),
            jnp.zeros((rows, 1), jnp.float32),
            jnp.zeros((rows, q_ref.shape[2]), jnp.float32),
        )
        m, l, acc = lax.fori_loop(0, (count + chunk - 1) // chunk, body, init)
        acc_out[slot] = acc
        m_out[slot] = m
        l_out[slot] = l


def cache_attention(q_blocks, keys, values, live, kv_local, group_size):
    reqs, rows, head_dim = q_blocks.shape
    flat_len = keys.shape[1]
    local_len = flat_len // kv_local
    chunk = min(256, local_len)
    rb = 2 if reqs % 2 == 0 else 1
    steps = reqs // rb
    step_ids = jnp.arange(steps, dtype=jnp.int32)
    step_live = jnp.max(live.reshape(steps, rb), axis=1) > 0
    kgrp = lax.cummax(jnp.where(step_live, step_ids, 0), axis=0)
    kernel = functools.partial(
        cache_kernel,
        rb=rb,
        chunk=chunk,
        kv_shift=log2_exact(kv_local),
        g_shift=log2_exact(group_size),
        scale=1.0 / math.sqrt(head_dim),
    )
    grid_spec = pltpu.PrefetchScalarGridSpec(
        num_scalar_prefetch=2,
        grid=(steps,),
        in_specs=[
            pl.BlockSpec((rb, rows, head_dim), lambda i, kg, lv: (i, 0, 0)),
            pl.BlockSpec((rb, flat_len, head_dim), lambda i, kg, lv: (kg[i], 0, 0)),
            pl.BlockSpec((rb, flat_len, head_dim), lambda i, kg, lv: (kg[i], 0, 0)),
        ],
        out_specs=[
            pl.BlockSpec((rb, rows, head_dim), lambda i, kg, lv: (i, 0, 0)),
            pl.BlockSpec((rb, rows, 1), lambda i, kg, lv: (i, 0, 0)),
            pl.BlockSpec((rb, rows, 1), lambda i, kg, lv: (i, 0, 0)),
        ],
    )
    return pl.pallas_call(
        kernel,
        grid_spec=grid_spec,
        out_shape=[
            jax.ShapeDtypeStruct((reqs, rows, head_dim), jnp.float32),
            jax.ShapeDtypeStruct((reqs, rows, 1), jnp.float32),
            jax.ShapeDtypeStruct((reqs, rows, 1), jnp.float32),
        ],
        compiler_params=pltpu.CompilerParams(dimension_semantics=("arbitrary",)),
    )(kgrp, live, q_blocks, keys, values)


def sum_over(part, axis):
    size = lax.axis_size(axis)
    split = part.reshape((size, part.shape[0] // size) + part.shape[1:])
    return jnp.sum(lax.all_to_all(split, axis, 0, 0).astype(jnp.float32), axis=0)


def on_device(
    tokens,
    q_weight,
    key_matrix,
    value_matrix,
    q_gain,
    key_norm_scale,
    stored_cache_keys,
    stored_cache_values,
    lengths,
    positions,
    o_weight,
):
    rows = tokens.shape[0]
    reqs, drafts = positions.shape
    kv_size = lax.axis_size("kv")
    kv_idx = lax.axis_index("kv")
    own_rows = rows // kv_size
    own_reqs = own_rows // drafts
    row0 = kv_idx * own_rows
    kv_local, head_dim = key_norm_scale.shape
    heads_local = q_gain.shape[0]
    group_size = heads_local // kv_local
    q_width = heads_local * head_dim
    k_width = kv_local * head_dim

    proj = jnp.concatenate(
        [
            jnp.dot(tokens, q_weight, preferred_element_type=jnp.float32),
            jnp.dot(tokens, key_matrix, preferred_element_type=jnp.float32),
            jnp.dot(tokens, value_matrix, preferred_element_type=jnp.float32),
        ],
        axis=1,
    )
    proj_own = sum_over(proj, "kv")
    pos_own = lax.dynamic_slice_in_dim(positions.reshape(rows), row0, own_rows)
    q_own = norm_rotate(proj_own[:, :q_width], q_gain, pos_own)
    k_own = norm_rotate(proj_own[:, q_width:q_width + k_width], key_norm_scale, pos_own)
    v_own = proj_own[:, q_width + k_width:].astype(jnp.bfloat16)
    query_rows = lax.all_gather(q_own, "kv", axis=0, tiled=True)

    local_len = stored_cache_keys.shape[1]
    offset = kv_idx * local_len
    live = jnp.clip(lengths - offset, 0, local_len).astype(jnp.int32)
    q_blocks = query_rows.reshape(reqs, drafts * heads_local, head_dim)
    keys = stored_cache_keys.reshape(reqs, local_len * kv_local, head_dim)
    values = stored_cache_values.reshape(reqs, local_len * kv_local, head_dim)
    acc_c, m_c, l_c = cache_attention(q_blocks, keys, values, live, kv_local, group_size)
    stat_pad = max(128, 2 * heads_local)
    packed = jnp.concatenate(
        [
            acc_c.reshape(rows, q_width),
            m_c.reshape(rows, heads_local),
            l_c.reshape(rows, heads_local),
            jnp.zeros((rows, stat_pad - 2 * heads_local), jnp.float32),
        ],
        axis=1,
    )
    packed = packed.reshape(kv_size, own_rows, q_width + stat_pad)
    gathered = lax.all_to_all(packed, "kv", 0, 0)
    acc_g = gathered[:, :, :q_width].reshape(kv_size, own_rows, heads_local, head_dim)
    m_g = gathered[:, :, q_width:q_width + heads_local]
    l_g = gathered[:, :, q_width + heads_local:q_width + 2 * heads_local]

    scale = 1.0 / math.sqrt(head_dim)
    q_d = q_own.reshape(own_reqs, drafts, kv_local, group_size, head_dim)
    k_d = k_own.reshape(own_reqs, drafts, kv_local, head_dim)
    v_d = v_own.reshape(own_reqs, drafts, kv_local, head_dim)
    s_d = jnp.einsum("rjkgd,rikd->rjkgi", q_d, k_d, preferred_element_type=jnp.float32) * scale
    pos_req = lax.dynamic_slice_in_dim(positions, kv_idx * own_reqs, own_reqs)
    order = jnp.arange(drafts, dtype=jnp.int32)
    seen = (order[None, :] == order[:, None])[None] | (order[None, :] < order[:, None])[None] & (
        pos_req[:, None, :] < pos_req[:, :, None]
    )
    mask_d = seen[:, :, None, None, :]
    s_d = jnp.where(mask_d, s_d, NEG)
    m_d = jnp.max(s_d, axis=-1)
    p_d = jnp.where(mask_d, jnp.exp(s_d - m_d[..., None]), 0.0)
    l_d = jnp.sum(p_d, axis=-1).reshape(own_rows, heads_local)
    acc_d = jnp.einsum(
        "rjkgi,rikd->rjkgd", p_d.astype(jnp.bfloat16), v_d, preferred_element_type=jnp.float32
    ).reshape(own_rows, heads_local, head_dim)
    m_d = m_d.reshape(own_rows, heads_local)

    top = jnp.maximum(jnp.max(m_g, axis=0), m_d)
    ratio = jnp.exp(m_g - top[None])
    ratio_d = jnp.exp(m_d - top)
    total = jnp.sum(l_g * ratio, axis=0) + l_d * ratio_d
    acc = jnp.sum(acc_g * ratio[..., None], axis=0) + acc_d * ratio_d[..., None]
    attended = (acc / total[..., None]).astype(jnp.bfloat16).reshape(own_rows, q_width)
    attended = lax.all_gather(attended, "kv", axis=0, tiled=True)
    partial_out = jnp.dot(attended, o_weight, preferred_element_type=jnp.float32)
    return sum_over(partial_out.astype(jnp.bfloat16), "head").astype(jnp.bfloat16)


def solution(mesh):
    placed = (
        P(None, "kv"),
        P("kv", "head"),
        P("kv", "head"),
        P("kv", "head"),
        P("head", None),
        P("head", None),
        P(None, "kv", "head", None),
        P(None, "kv", "head", None),
        P(),
        P(),
        P("head", "kv"),
    )
    return jax.shard_map(
        on_device, mesh=mesh, in_specs=placed, out_specs=P("head", "kv"), check_vma=False
    )
```

time: 296 us -> 138 us (0.47)
  waiting for transfers between devices: 156 us -> 31.4 us
  Pallas kernels: 55.2 us -> 37.6 us
  between operations: 13.8 us -> 0.35 us
  blocking collectives: 42.3 us -> 30.1 us
  starting transfers between devices: 0.21 us -> 9.67 us
  local copies, waits for them, and re-layouts: 4.45 us -> 10.5 us
  matrix products: 9.19 us -> 4.55 us
    reduce_scatter x6 -> x0, waiting for transfers between devices: 156 us -> none  [the longest x3 69.4 us: on_device(): lax.psum_scatter((q_part, k_part, v_part), 'kv', scatter_dimension=0, til...]
    all_to_all x0 -> x2, waiting for transfers between devices: none -> 31.4 us  [the longest x1 16.7 us: sum_over(): lax.all_to_all(split, axis, 0, 0).astype(jnp.float32)]
    pmax x1 -> x0, blocking collectives: 22.7 us -> none  [on_device(): top = lax.pmax(m_all, 'kv')]
    pallas_call x1, Pallas kernels: 55.2 us -> 37.6 us  [cache_attention(): pl.pallas_call(kernel, grid_spec=grid_spec, out_shape=[jax.ShapeDtypeStru...]
    all_to_all x0 -> x1, blocking collectives: none -> 12.3 us  [sum_over(): lax.all_to_all(split, axis, 0, 0).astype(jnp.float32)]
    all_to_all x0 -> x2, starting transfers between devices: none -> 9.67 us  [the longest x1 5.3 us: sum_over(): lax.all_to_all(split, axis, 0, 0).astype(jnp.float32)]
    reduce_sum x0 -> x4, other arithmetic: none -> 4.85 us  [the longest x2 2.04 us: sum_over(): jnp.sum(lax.all_to_all(split, axis, 0, 0).astype(jnp.float32), axis=0)]
    concatenate x0 -> x4, local copies, waits for them, and re-layouts: none -> 4.7 us  [on_device(): jnp.concatenate([acc_c.reshape(rows, q_width), m_c.reshape(rows, heads_lo...]
  transfers between devices with their start and end apart: 6 -> 2, of which waited for: 5 -> 2; matrix products, arithmetic and copies ran while one was open for 6% -> 2% of each run, Pallas kernels for 19% -> 0%
where the time goes in v2:
time: 138 us; the launch traced here: 136 us
  Pallas kernels  37.6 us (27%)
  waiting for transfers between devices  31.4 us (23%)
  blocking collectives  30.1 us (22%)
  other arithmetic  12.1 us (9%)
  local copies, waits for them, and re-layouts  10.5 us (8%)
  starting transfers between devices  9.67 us (7%)
  matrix products  4.55 us (3%)
    pallas_call x1, Pallas kernels, cache_attention(): pl.pallas_call(kernel, grid_spec=grid_spec, out_shape=[jax.ShapeDtypeStru...  37.6 us
    all_to_all x1, waiting for transfers between devices, sum_over(): lax.all_to_all(split, axis, 0, 0).astype(jnp.float32)  16.7 us
    all_to_all x1, waiting for transfers between devices, on_device(): gathered = lax.all_to_all(packed, 'kv', 0, 0)  14.7 us
    all_to_all x1, blocking collectives, sum_over(): lax.all_to_all(split, axis, 0, 0).astype(jnp.float32)  12.3 us
    all_gather x1, blocking collectives, on_device(): query_rows = lax.all_gather(q_own, 'kv', axis=0, tiled=True)  8.91 us
    all_gather x1, blocking collectives, on_device(): attended = lax.all_gather(attended, 'kv', axis=0, tiled=True)  8.89 us
    all_to_all x1, starting transfers between devices, sum_over(): lax.all_to_all(split, axis, 0, 0).astype(jnp.float32)  5.3 us
    concatenate x4, local copies, waits for them, and re-layouts, on_device(): jnp.concatenate([acc_c.reshape(rows, q_width), m_c.reshape(rows, heads_lo...  4.7 us
  transfers between devices with their start and end apart: 2, of which 2 were waited for; matrix products, arithmetic and copies ran while one was open for 2% of the time, Pallas kernels for 0%

profile of v2, /device:TPU:0, one launch (start us, length us, event | category | flops | bytes accessed | tf_op | source)
XLA Modules:
  0.0 136.3 jit_solution(8528559067923218916)
XLA Ops:
  0.0 1.4 %fusion.18 = f32[128,256]{1,0:T(8,128)S(1)} fusion(bf16[128,640]{1,0:T(8,128)(2,1)} %param.11, bf16[640,256]{1,0:T(8,128)(2,1)} %param.13), kind=kOutput, calls=%fused_computation.55 | convolution fusion | flops 41943040 | bytes 622592 | tf_op jit(solution)/shard_map/dot_general | solution.py:160
  1.4 1.3 fusion.19
  2.7 0.6 fusion.17
  3.3 1.2 pad_maximum_fusion
  4.5 5.3 %all-to-all-start = ((f32[8,16,2560]{2,1,0:T(8,128)}), f32[8,16,2560]{2,1,0:T(8,128)}, u32[]{:S(2)}, u32[]{:S(2)}) async-start(f32[8,16,2560]{2,1,0:T(8,128)} %bitcast.51), calls=%async_computation | async-start | bytes 2621440 | tf_op jit(solution)/shard_map/all_to_all | solution.py:128
  9.8 0.1 copy.46
  10.0 0.1 copy.47
  10.2 0.1 reduce_max.27
  10.3 0.1 copy.45
  10.4 0.6 reduce.2.kgrp
  11.1 0.1 reshape.251
  11.2 0.1 dynamic-slice_convert_fusion
  11.4 0.1 multiply_cosine_fusion
  11.5 16.7 %all-to-all-done = f32[8,16,2560]{2,1,0:T(8,128)} async-done(((f32[8,16,2560]{2,1,0:T(8,128)}), f32[8,16,2560]{2,1,0:T(8,128)}, u32[]{:S(2)}, u32[]{:S(2)}) %all-to-all-start) | async-done | bytes 1310752 | tf_op jit(solution)/shard_map/all_to_all | solution.py:128
  28.1 1.4 %reduce_sum.66 = f32[16,2560]{1,0:T(8,128)S(1)} reduce(f32[8,16,2560]{2,1,0:T(8,128)} %all-to-all-done, f32[]{:T(128)} %constant.8.clone.1), dimensions={0}, to_apply=%region_2.0 | reduce | flops 286720 | bytes 1474564 | tf_op jit(solution)/shard_map/reduce_sum | solution.py:128
  29.6 0.1 multiply_reduce_fusion
  29.7 0.1 multiply_reduce_fusion.1
  29.9 0.1 multiply_multiply_fusion
  30.0 0.1 multiply_subtract_fusion
  30.1 0.1 maximum_convert_fusion
  30.2 8.9 %all_gather.6 = bf16[128,2048]{1,0:T(8,128)(2,1)S(1)} all-gather(bf16[16,2048]{1,0:T(8,128)(2,1)S(1)} %bitcast.58), channel_id=1, replica_groups=mesh['kv'=8,'head'=4] {'kv'}, dimensions={0}, use_global_device_ids=true | all-gather | bytes 589824 | tf_op jit(solution)/shard_map/all_gather | solution.py:170
  39.1 1.0 reshape.252.q_ref
  40.1 37.6 %shard_map.109 = (f32[32,64,128]{2,1,0:T(8,128)}, f32[32,64,1]{2,1,0:T(8,128)}, f32[32,64,1]{2,1,0:T(8,128)}) custom-call(s32[16]{0:T(128)} %reduce.2.kgrp, s32[32]{0:T(128)} %copy-done.5, bf16[32,64,128]{2,1,0:T(8,128)(2,1)} %reshape.252.q_ref, bf16[32,2048,128]{2,1,0:T(8,128)(2,1)} %bitcast.49, bf16[32,2048,128]{2,1,0:T(8,128)(2,1)} %bitcast.50), custom_call_target="tpu_custom_call" | custom-call | tf_op jit(solution)/shard_map/pallas_call | solution.py:113
  77.7 2.4 %concatenate.22 = f32[8,16,2048]{2,1,0:T(8,128)} reshape(f32[32,64,128]{2,1,0:T(8,128)} %get-tuple-element.8) | data formatting | bytes 2097152 | tf_op jit(solution)/shard_map/concatenate | solution.py:180
  80.1 1.6 %reduce.3 = f32[32,64]{1,0:T(8,128)S(1)} reduce(f32[32,64,1]{2,1,0:T(8,128)} %get-tuple-element.9, f32[]{:T(128)} %constant.53), dimensions={2}, to_apply=%get-tuple-element.9.reduce_sub_computation | reduce | bytes 16388 | tf_op jit(solution)/shard_map/pallas_call | solution.py:113
  81.6 1.6 %reduce.4 = f32[32,64]{1,0:T(8,128)S(1)} reduce(f32[32,64,1]{2,1,0:T(8,128)} %get-tuple-element.10, f32[]{:T(128)} %constant.53), dimensions={2}, to_apply=%get-tuple-element.10.reduce_sub_computation | reduce | bytes 16388 | tf_op jit(solution)/shard_map/pallas_call | solution.py:113
  83.4 2.2 %concatenate.25 = f32[8,16,2176]{2,1,0:T(8,128)} concatenate(f32[8,16,2048]{2,1,0:T(8,128)} %concatenate.22, f32[8,16,16]{2,1,0:T(8,128)S(1)} %concatenate.23, f32[8,16,16]{2,1,0:T(8,128)S(1)} %concatenate.24, f32[8,16,96]{2,1,0:T(8,128)S(1)} %broadcast_in_dim.18), dimensions={2} | concatenate | bytes 2228224 | tf_op jit(solution)/shard_map/concatenate | solution.py:180
  85.6 4.4 %all-to-all-start.1 = ((f32[8,16,2176]{2,1,0:T(8,128)}), f32[8,16,2176]{2,1,0:T(8,128)}, u32[]{:S(2)}, u32[]{:S(2)}) async-start(f32[8,16,2176]{2,1,0:T(8,128)} %concatenate.25), calls=%async_computation.1 | async-start | bytes 2228224 | tf_op jit(solution)/shard_map/all_to_all | solution.py:190
  90.0 0.1 multiply_multiply_fusion.1
  90.1 0.1 subtract_convert_fusion
  90.2 0.1 pad_maximum_fusion.1
  90.3 0.4 fusion.16
  90.7 0.1 fusion.7
  90.9 0.1 reshape.259
  91.0 0.3 convolution_bitcast_fusion
  91.3 14.7 %all-to-all-done.1 = f32[8,16,2176]{2,1,0:T(8,128)} async-done(((f32[8,16,2176]{2,1,0:T(8,128)}), f32[8,16,2176]{2,1,0:T(8,128)}, u32[]{:S(2)}, u32[]{:S(2)}) %all-to-all-start.1) | async-done | bytes 1114144 | tf_op jit(solution)/shard_map/all_to_all | solution.py:190
  106.1 0.9 slice_reduce_fusion
  106.9 1.0 fusion.5
  108.0 1.3 mul.206
  109.3 2.4 %mul.207 = f32[8,16,2048]{2,1,0:T(8,128)} reshape(f32[8,16,16,128]{3,2,1,0:T(8,128)} %mul.206) | data formatting | bytes 2097152 | tf_op jit(solution)/shard_map/mul | solution.py:219
  111.7 1.8 %fusion.2 = f32[16,2048]{1,0:T(8,128)S(1)} fusion(f32[8,16,2048]{2,1,0:T(8,128)} %mul.207, f32[8,16,2176]{2,1,0:T(8,128)} %all-to-all-done.1), kind=kLoop, calls=%fused_computation.7 | loop fusion | flops 491520 | bytes 2228224 | tf_op jit(solution)/shard_map/reduce_sum | solution.py:219
  113.5 0.1 div.35
  113.6 0.1 mul.209
  113.7 0.1 fusion.3
  113.8 8.9 %all_gather.7 = bf16[128,2048]{1,0:T(8,128)(2,1)S(1)} all-gather(bf16[16,2048]{1,0:T(8,128)(2,1)S(1)} %fusion.3), channel_id=1, replica_groups=mesh['kv'=8,'head'=4] {'kv'}, dimensions={0}, use_global_device_ids=true | all-gather | bytes 589824 | tf_op jit(solution)/shard_map/all_gather | solution.py:221
  122.7 0.6 convolution_convert_fusion
  123.3 12.3 %all_to_all.15 = bf16[4,32,640]{2,1,0:T(8,128)(2,1)S(1)} all-to-all(bf16[4,32,640]{2,1,0:T(8,128)(2,1)S(1)} %bitcast.53), channel_id=1, replica_groups=mesh['kv'=8,'head'=4] {'head'}, dimensions={0} | all-to-all | bytes 327680 | tf_op jit(solution)/shard_map/all_to_all | solution.py:128
  135.6 0.6 reduce_sum.72
  (43 shorter events, 0.7 us)
Async XLA Ops:
  0.0 2.7 %copy-start = (bf16[640,2048]{1,0:T(8,128)(2,1)S(1)}, bf16[640,2048]{1,0:T(8,128)(2,1)}, u32[]{:S(2)}) copy-start(bf16[640,2048]{1,0:T(8,128)(2,1)} %param.12) | copy-start | bytes 7864324
  0.0 2.7 %copy-start.2 = (bf16[128,640]{1,0:T(8,128)(2,1)S(1)}, bf16[128,640]{1,0:T(8,128)(2,1)}, u32[]{:S(2)}) copy-start(bf16[128,640]{1,0:T(8,128)(2,1)} %param.11) | copy-start | bytes 491524
  4.5 5.3 %copy-start.4 = (s32[32,4]{0,1:T(4,128)S(1)}, s32[32,4]{0,1:T(4,128)}, u32[]{:S(2)}) copy-start(s32[32,4]{0,1:T(4,128)} %param.20) | copy-start | bytes 1540
  4.5 5.6 %copy-start.7 = (s32[32]{0:T(128)S(1)}, s32[32]{0:T(128)}, u32[]{:S(2)}) copy-start(s32[32]{0:T(128)} %param.19) | copy-start | bytes 388
  4.5 23.6 %all-to-all-start = ((f32[8,16,2560]{2,1,0:T(8,128)}), f32[8,16,2560]{2,1,0:T(8,128)}, u32[]{:S(2)}, u32[]{:S(2)}) async-start(f32[8,16,2560]{2,1,0:T(8,128)} %bitcast.51), calls=%async_computation | async-start | bytes 2621440 | tf_op jit(solution)/shard_map/all_to_all | solution.py:128
  9.8 20.0 %copy-start.3 = (f32[16,128]{1,0:T(8,128)S(1)}, f32[16,128]{1,0:T(8,128)}, u32[]{:S(2)}) copy-start(f32[16,128]{1,0:T(8,128)} %param.15) | copy-start | bytes 24580
  10.1 19.9 %copy-start.5 = (s32[32]{0:T(128)}, s32[32]{0:T(128)S(1)}, u32[]{:S(2)}) copy-start(s32[32]{0:T(128)S(1)} %subtract_clamp_fusion.live) | copy-start | bytes 388
  85.6 4.4 %copy-start.6 = (f32[2,128]{1,0:T(2,128)S(1)}, f32[2,128]{1,0:T(2,128)}, u32[]{:S(2)}) copy-start(f32[2,128]{1,0:T(2,128)} %param.16) | copy-start | bytes 3076
  85.6 20.5 %all-to-all-start.1 = ((f32[8,16,2176]{2,1,0:T(8,128)}), f32[8,16,2176]{2,1,0:T(8,128)}, u32[]{:S(2)}, u32[]{:S(2)}) async-start(f32[8,16,2176]{2,1,0:T(8,128)} %concatenate.25), calls=%async_computation.1 | async-start | bytes 2228224 | tf_op jit(solution)/shard_map/all_to_all | solution.py:190
  111.7 11.0 %copy-start.1 = (bf16[2048,640]{1,0:T(8,128)(2,1)S(1)}, bf16[2048,640]{1,0:T(8,128)(2,1)}, u32[]{:S(2)}) copy-start(bf16[2048,640]{1,0:T(8,128)(2,1)} %param.21) | copy-start | bytes 7864324

commit v3 on v2

--- a/solution.py
+++ b/solution.py
@@ -35,7 +35,7 @@
     return shift
 
 
-def cache_kernel(kgrp, live, q_ref, k_ref, v_ref, acc_out, m_out, l_out,
+def cache_kernel(kgrp, live, q_ref, k_ref, v_ref, out_ref,
                  *, rb, chunk, kv_shift, g_shift, scale):
     step = pl.program_id(0)
     rows = q_ref.shape[1]
@@ -45,6 +45,7 @@
     row = lax.broadcasted_iota(jnp.int32, (rows, width), 0)
     same_head = (col & kv_mask) == ((row >> g_shift) & kv_mask)
     col_pos = col >> kv_shift
+    lanes = out_ref.shape[2]
     for slot in range(rb):
         count = live[step * rb + slot]
         q = q_ref[slot]
@@ -73,13 +74,17 @@
             jnp.zeros((rows, q_ref.shape[2]), jnp.float32),
         )
         m, l, acc = lax.fori_loop(0, (count + chunk - 1) // chunk, body, init)
-        acc_out[slot] = acc
-        m_out[slot] = m
-        l_out[slot] = l
+        out_ref[slot, :rows, :] = acc
+        pieces = [jnp.broadcast_to(m, (rows, lanes)), jnp.broadcast_to(l, (rows, lanes))]
+        if lanes > 2 * rows:
+            pieces.append(jnp.zeros((lanes - 2 * rows, lanes), jnp.float32))
+        stacked = jnp.concatenate(pieces, axis=0)
+        out_ref[slot, rows:, :] = jnp.transpose(stacked)[: out_ref.shape[1] - rows, :]
 
 
 def cache_attention(q_blocks, keys, values, live, kv_local, group_size):
     reqs, rows, head_dim = q_blocks.shape
+    assert 2 * rows <= head_dim
     flat_len = keys.shape[1]
     local_len = flat_len // kv_local
     chunk = min(256, local_len)
@@ -96,6 +101,7 @@
         g_shift=log2_exact(group_size),
         scale=1.0 / math.sqrt(head_dim),
     )
+    out_rows = rows + 8
     grid_spec = pltpu.PrefetchScalarGridSpec(
         num_scalar_prefetch=2,
         grid=(steps,),
@@ -104,20 +110,12 @@
             pl.BlockSpec((rb, flat_len, head_dim), lambda i, kg, lv: (kg[i], 0, 0)),
             pl.BlockSpec((rb, flat_len, head_dim), lambda i, kg, lv: (kg[i], 0, 0)),
         ],
-        out_specs=[
-            pl.BlockSpec((rb, rows, head_dim), lambda i, kg, lv: (i, 0, 0)),
-            pl.BlockSpec((rb, rows, 1), lambda i, kg, lv: (i, 0, 0)),
-            pl.BlockSpec((rb, rows, 1), lambda i, kg, lv: (i, 0, 0)),
-        ],
+        out_specs=pl.BlockSpec((rb, out_rows, head_dim), lambda i, kg, lv: (i, 0, 0)),
     )
     return pl.pallas_call(
         kernel,
         grid_spec=grid_spec,
-        out_shape=[
-            jax.ShapeDtypeStruct((reqs, rows, head_dim), jnp.float32),
-            jax.ShapeDtypeStruct((reqs, rows, 1), jnp.float32),
-            jax.ShapeDtypeStruct((reqs, rows, 1), jnp.float32),
-        ],
+        out_shape=jax.ShapeDtypeStruct((reqs, out_rows, head_dim), jnp.float32),
         compiler_params=pltpu.CompilerParams(dimension_semantics=("arbitrary",)),
     )(kgrp, live, q_blocks, keys, values)
 
@@ -167,30 +165,23 @@
     q_own = norm_rotate(proj_own[:, :q_width], q_gain, pos_own)
     k_own = norm_rotate(proj_own[:, q_width:q_width + k_width], key_norm_scale, pos_own)
     v_own = proj_own[:, q_width + k_width:].astype(jnp.bfloat16)
-    query_rows = lax.all_gather(q_own, "kv", axis=0, tiled=True)
+    rows_r = drafts * heads_local
+    q_blocks = lax.all_gather(
+        q_own.reshape(own_reqs, rows_r, head_dim), "kv", axis=0, tiled=True
+    )
 
     local_len = stored_cache_keys.shape[1]
     offset = kv_idx * local_len
     live = jnp.clip(lengths - offset, 0, local_len).astype(jnp.int32)
-    q_blocks = query_rows.reshape(reqs, drafts * heads_local, head_dim)
     keys = stored_cache_keys.reshape(reqs, local_len * kv_local, head_dim)
     values = stored_cache_values.reshape(reqs, local_len * kv_local, head_dim)
-    acc_c, m_c, l_c = cache_attention(q_blocks, keys, values, live, kv_local, group_size)
-    stat_pad = max(128, 2 * heads_local)
-    packed = jnp.concatenate(
-        [
-            acc_c.reshape(rows, q_width),
-            m_c.reshape(rows, heads_local),
-            l_c.reshape(rows, heads_local),
-            jnp.zeros((rows, stat_pad - 2 * heads_local), jnp.float32),
-        ],
-        axis=1,
-    )
-    packed = packed.reshape(kv_size, own_rows, q_width + stat_pad)
-    gathered = lax.all_to_all(packed, "kv", 0, 0)
-    acc_g = gathered[:, :, :q_width].reshape(kv_size, own_rows, heads_local, head_dim)
-    m_g = gathered[:, :, q_width:q_width + heads_local]
-    l_g = gathered[:, :, q_width + heads_local:q_width + 2 * heads_local]
+    partial = cache_attention(q_blocks, keys, values, live, kv_local, group_size)
+    gathered = lax.all_to_all(
+        partial.reshape((kv_size, own_reqs) + partial.shape[1:]), "kv", 0, 0
+    )
+    acc_g = gathered[:, :, :rows_r, :]
+    m_g = gathered[:, :, rows_r, :rows_r]
+    l_g = gathered[:, :, rows_r, rows_r:2 * rows_r]
 
     scale = 1.0 / math.sqrt(head_dim)
     q_d = q_own.reshape(own_reqs, drafts, kv_local, group_size, head_dim)
@@ -206,11 +197,11 @@
     s_d = jnp.where(mask_d, s_d, NEG)
     m_d = jnp.max(s_d, axis=-1)
     p_d = jnp.where(mask_d, jnp.exp(s_d - m_d[..., None]), 0.0)
-    l_d = jnp.sum(p_d, axis=-1).reshape(own_rows, heads_local)
+    l_d = jnp.sum(p_d, axis=-1).reshape(own_reqs, rows_r)
     acc_d = jnp.einsum(
         "rjkgi,rikd->rjkgd", p_d.astype(jnp.bfloat16), v_d, preferred_element_type=jnp.float32
-    ).reshape(own_rows, heads_local, head_dim)
-    m_d = m_d.reshape(own_rows, heads_local)
+    ).reshape(own_reqs, rows_r, head_dim)
+    m_d = m_d.reshape(own_reqs, rows_r)
 
     top = jnp.maximum(jnp.max(m_g, axis=0), m_d)
     ratio = jnp.exp(m_g - top[None])

time: 138 us -> 125 us (0.906)
  local copies, waits for them, and re-layouts: 10.5 us -> 2.2 us
  other arithmetic: 12.1 us -> 6.87 us
  Pallas kernels: 37.6 us -> 34.2 us
  matrix products: 4.55 us -> 6.29 us
    concatenate x4 -> x0, local copies, waits for them, and re-layouts: 4.7 us -> none  [on_device(): jnp.concatenate([acc_c.reshape(rows, q_width), m_c.reshape(rows, heads_lo...]
    mul x3 -> x2, local copies, waits for them, and re-layouts: 3.82 us -> 0.12 us  [on_device(): acc = jnp.sum(acc_g * ratio[..., None], axis=0) + acc_d * ratio_d[..., None]]
    pallas_call x1, Pallas kernels: 37.6 us -> 34.2 us  [cache_attention(): pl.pallas_call(kernel, grid_spec=grid_spec, out_shape=jax.ShapeDtypeStruc...]
    pallas_call x2 -> x0, other arithmetic: 3.14 us -> none  [cache_attention(): pl.pallas_call(kernel, grid_spec=grid_spec, out_shape=[jax.ShapeDtypeStru...]
    dot_general x1, matrix products: 0.58 us -> 2.32 us  [on_device(): jnp.dot(attended, o_weight, preferred_element_type=jnp.float32)]
where the time goes in v3:
time: 125 us; the launch traced here: 123 us
  Pallas kernels  34.2 us (27%)
  waiting for transfers between devices  31.9 us (26%)
  blocking collectives  31.2 us (25%)
  starting transfers between devices  9.71 us (8%)
  other arithmetic  6.87 us (5%)
  matrix products  6.29 us (5%)
  local copies, waits for them, and re-layouts  2.2 us (2%)
    pallas_call x1, Pallas kernels, cache_attention(): pl.pallas_call(kernel, grid_spec=grid_spec, out_shape=jax.ShapeDtypeStruc...  34.2 us
    all_to_all x1, waiting for transfers between devices, sum_over(): lax.all_to_all(split, axis, 0, 0).astype(jnp.float32)  16.6 us
    all_to_all x1, waiting for transfers between devices, on_device(): lax.all_to_all(partial.reshape((kv_size, own_reqs) + partial.shape[1:]),...  15.3 us
    all_to_all x1, blocking collectives, sum_over(): lax.all_to_all(split, axis, 0, 0).astype(jnp.float32)  12.3 us
    all_gather x1, blocking collectives, on_device(): lax.all_gather(q_own.reshape(own_reqs, rows_r, head_dim), 'kv', axis=0, t...  9.93 us
    all_gather x1, blocking collectives, on_device(): attended = lax.all_gather(attended, 'kv', axis=0, tiled=True)  8.89 us
    all_to_all x1, starting transfers between devices, sum_over(): lax.all_to_all(split, axis, 0, 0).astype(jnp.float32)  5.3 us
    all_to_all x1, starting transfers between devices, on_device(): lax.all_to_all(partial.reshape((kv_size, own_reqs) + partial.shape[1:]),...  4.4 us
  transfers between devices with their start and end apart: 2, of which 2 were waited for; matrix products, arithmetic and copies ran while one was open for 2% of the time, Pallas kernels for 0%

profile of v3, /device:TPU:0, one launch (start us, length us, event | category | flops | bytes accessed | tf_op | source)
XLA Modules:
  0.0 122.7 jit_solution(1213254421364838020)
XLA Ops:
  0.0 0.0 copy-start
  0.0 1.4 %fusion.17 = f32[128,256]{1,0:T(8,128)S(1)} fusion(bf16[128,640]{1,0:T(8,128)(2,1)} %param.11, bf16[640,256]{1,0:T(8,128)(2,1)} %param.14), kind=kOutput, calls=%fused_computation.51 | convolution fusion | flops 41943040 | bytes 622592 | tf_op jit(solution)/shard_map/dot_general | solution.py:159
  1.4 1.3 %fusion.16 = f32[128,256]{1,0:T(8,128)S(1)} fusion(bf16[128,640]{1,0:T(8,128)(2,1)} %param.11, bf16[640,256]{1,0:T(8,128)(2,1)} %param.13), kind=kOutput, calls=%fused_computation.50 | convolution fusion | flops 41943040 | bytes 622592 | tf_op jit(solution)/shard_map/dot_general | solution.py:158
  2.7 0.0 copy-done
  2.7 0.6 fusion.15
  3.3 1.2 pad_maximum_fusion
  4.5 5.3 %all-to-all-start = ((f32[8,16,2560]{2,1,0:T(8,128)}), f32[8,16,2560]{2,1,0:T(8,128)}, u32[]{:S(2)}, u32[]{:S(2)}) async-start(f32[8,16,2560]{2,1,0:T(8,128)} %bitcast.39), calls=%async_computation | async-start | bytes 2621440 | tf_op jit(solution)/shard_map/all_to_all | solution.py:126
  9.8 0.0 copy-done.7
  9.8 0.0 copy-start.5
  9.8 0.1 reshape.239
  9.9 0.1 reduce_max.27
  10.1 0.1 copy.49
  10.2 0.1 copy.50
  10.3 0.1 reshape.243
  10.4 0.6 reduce.2.kgrp
  11.0 0.1 constant_dynamic-slice_fusion
  11.1 0.1 copy.52
  11.2 0.1 dynamic-slice_convert_fusion
  11.3 0.1 and_or_fusion
  11.4 0.1 multiply_cosine_fusion
  11.5 16.6 %all-to-all-done = f32[8,16,2560]{2,1,0:T(8,128)} async-done(((f32[8,16,2560]{2,1,0:T(8,128)}), f32[8,16,2560]{2,1,0:T(8,128)}, u32[]{:S(2)}, u32[]{:S(2)}) %all-to-all-start) | async-done | bytes 1310752 | tf_op jit(solution)/shard_map/all_to_all | solution.py:126
  28.1 1.4 %reduce_sum.68 = f32[16,2560]{1,0:T(8,128)S(1)} reduce(f32[8,16,2560]{2,1,0:T(8,128)} %all-to-all-done, f32[]{:T(128)} %constant.9.clone.1), dimensions={0}, to_apply=%region_2.0 | reduce | flops 286720 | bytes 1474564 | tf_op jit(solution)/shard_map/reduce_sum | solution.py:126
  29.6 0.1 multiply_reduce_fusion
  29.7 0.0 copy-done.3
  29.7 0.1 multiply_multiply_fusion
  29.9 0.1 multiply_subtract_fusion
  30.0 0.1 maximum_convert_fusion
  30.1 9.9 %all_gather.6.q_ref = bf16[32,64,128]{2,1,0:T(8,128)(2,1)} all-gather(bf16[4,64,128]{2,1,0:T(8,128)(2,1)S(1)} %bitcast.43), channel_id=1, replica_groups=mesh['kv'=8,'head'=4] {'kv'}, dimensions={0}, use_global_device_ids=true | all-gather | bytes 589824 | tf_op jit(solution)/shard_map/all_gather | solution.py:169
  40.0 34.2 %shard_map.109 = f32[32,72,128]{2,1,0:T(8,128)} custom-call(s32[16]{0:T(128)} %reduce.2.kgrp, s32[32]{0:T(128)} %copy-done.5, bf16[32,64,128]{2,1,0:T(8,128)(2,1)} %all_gather.6.q_ref, bf16[32,2048,128]{2,1,0:T(8,128)(2,1)} %bitcast.37, bf16[32,2048,128]{2,1,0:T(8,128)(2,1)} %bitcast.38), custom_call_target="tpu_custom_call" | custom-call | tf_op jit(solution)/shard_map/pallas_call | solution.py:115
  74.2 4.4 %all-to-all-start.1 = ((f32[8,4,72,128]{3,2,1,0:T(8,128)}), f32[8,4,72,128]{3,2,1,0:T(8,128)}, u32[]{:S(2)}, u32[]{:S(2)}) async-start(f32[8,4,72,128]{3,2,1,0:T(8,128)} %bitcast.40), calls=%async_computation.1 | async-start | bytes 2359296 | tf_op jit(solution)/shard_map/all_to_all | solution.py:179
  78.7 0.1 multiply_reduce_fusion.2
  78.8 0.1 multiply_multiply_fusion.1
  78.9 0.1 subtract_convert_fusion
  79.0 0.1 pad_maximum_fusion.1
  79.0 0.4 fusion.14
  79.5 0.1 reshape.248
  79.6 0.1 fusion.4
  79.7 0.1 reshape.251
  79.8 0.3 convolution_bitcast_fusion
  80.2 15.3 %all-to-all-done.1 = f32[8,4,72,128]{3,2,1,0:T(8,128)} async-done(((f32[8,4,72,128]{3,2,1,0:T(8,128)}), f32[8,4,72,128]{3,2,1,0:T(8,128)}, u32[]{:S(2)}, u32[]{:S(2)}) %all-to-all-start.1) | async-done | bytes 1179680 | tf_op jit(solution)/shard_map/all_to_all | solution.py:179
  95.4 1.1 fusion.13
  96.6 0.1 div.35
  96.7 1.6 %fusion.2 = f32[4,64,128]{2,1,0:T(8,128)S(1)} fusion(f32[8,4,72,128]{3,2,1,0:T(8,128)} %all-to-all-done.1, f32[8,4,64]{2,1,0:T(4,128)S(1)} %get-tuple-element.8), kind=kLoop, calls=%fused_computation.7 | loop fusion | flops 491520 | bytes 1187840 | tf_op jit(solution)/shard_map/reduce_sum | solution.py:210
  98.4 0.1 mul.205
  98.5 8.9 %all_gather.7 = bf16[128,2048]{1,0:T(8,128)(2,1)S(1)} all-gather(bf16[16,2048]{1,0:T(8,128)(2,1)S(1)} %divide_convert_fusion), channel_id=1, replica_groups=mesh['kv'=8,'head'=4] {'kv'}, dimensions={0}, use_global_device_ids=true | all-gather | bytes 589824 | tf_op jit(solution)/shard_map/all_gather | solution.py:212
  107.4 2.3 %convolution_convert_fusion = bf16[128,640]{1,0:T(8,128)(2,1)S(1)} fusion(bf16[128,2048]{1,0:T(8,128)(2,1)S(1)} %all_gather.7, bf16[2048,640]{1,0:T(8,128)(2,1)} %param.21), kind=kOutput, calls=%fused_computation.1 | convolution fusion | flops 335626240 | bytes 3309568 | tf_op jit(solution)/shard_map/dot_general | solution.py:213
  109.7 12.3 %all_to_all.15 = bf16[4,32,640]{2,1,0:T(8,128)(2,1)S(1)} all-to-all(bf16[4,32,640]{2,1,0:T(8,128)(2,1)S(1)} %bitcast.42), channel_id=1, replica_groups=mesh['kv'=8,'head'=4] {'head'}, dimensions={0} | all-to-all | bytes 327680 | tf_op jit(solution)/shard_map/all_to_all | solution.py:126
  122.1 0.6 reduce_sum.75
  (37 shorter events, 0.4 us)
Async XLA Ops:
  0.0 2.7 %copy-start = (bf16[640,2048]{1,0:T(8,128)(2,1)S(1)}, bf16[640,2048]{1,0:T(8,128)(2,1)}, u32[]{:S(2)}) copy-start(bf16[640,2048]{1,0:T(8,128)(2,1)} %param.12) | copy-start | bytes 7864324
  0.0 2.7 %copy-start.1 = (bf16[128,640]{1,0:T(8,128)(2,1)S(1)}, bf16[128,640]{1,0:T(8,128)(2,1)}, u32[]{:S(2)}) copy-start(bf16[128,640]{1,0:T(8,128)(2,1)} %param.11) | copy-start | bytes 491524
  4.5 5.3 %copy-start.7 = (s32[32]{0:T(128)S(1)}, s32[32]{0:T(128)}, u32[]{:S(2)}) copy-start(s32[32]{0:T(128)} %param.19) | copy-start | bytes 388
  4.5 5.7 %copy-start.4 = (s32[32,4]{0,1:T(4,128)S(1)}, s32[32,4]{0,1:T(4,128)}, u32[]{:S(2)}) copy-start(s32[32,4]{0,1:T(4,128)} %param.20) | copy-start | bytes 1540
  4.5 23.6 %all-to-all-start = ((f32[8,16,2560]{2,1,0:T(8,128)}), f32[8,16,2560]{2,1,0:T(8,128)}, u32[]{:S(2)}, u32[]{:S(2)}) async-start(f32[8,16,2560]{2,1,0:T(8,128)} %bitcast.39), calls=%async_computation | async-start | bytes 2621440 | tf_op jit(solution)/shard_map/all_to_all | solution.py:126
  9.8 19.9 %copy-start.3 = (f32[16,128]{1,0:T(8,128)S(1)}, f32[16,128]{1,0:T(8,128)}, u32[]{:S(2)}) copy-start(f32[16,128]{1,0:T(8,128)} %param.15) | copy-start | bytes 24580
  9.8 20.0 %copy-start.5 = (s32[32]{0:T(128)}, s32[32]{0:T(128)S(1)}, u32[]{:S(2)}) copy-start(s32[32]{0:T(128)S(1)} %subtract_clamp_fusion.live) | copy-start | bytes 388
  29.5 44.7 %copy-start.2 = (f32[16,2560]{1,0:T(8,128)}, f32[16,2560]{1,0:T(8,128)S(1)}, u32[]{:S(2)}) copy-start(f32[16,2560]{1,0:T(8,128)S(1)} %reduce_sum.68) | copy-start | bytes 491524
  74.2 4.6 %copy-start.6 = (f32[2,128]{1,0:T(2,128)S(1)}, f32[2,128]{1,0:T(2,128)}, u32[]{:S(2)}) copy-start(f32[2,128]{1,0:T(2,128)} %param.16) | copy-start | bytes 3076
  74.2 4.4 %slice-start = ((f32[16,2560]{1,0:T(8,128)}), f32[16,256]{1,0:T(8,128)S(1)}, s32[]{:S(2)}) async-start(f32[16,2560]{1,0:T(8,128)} %copy-done.2), calls=%async_computation.3 | async-start | bytes 32768 | tf_op jit(solution)/shard_map/slice | solution.py:166
  74.2 21.2 %all-to-all-start.1 = ((f32[8,4,72,128]{3,2,1,0:T(8,128)}), f32[8,4,72,128]{3,2,1,0:T(8,128)}, u32[]{:S(2)}, u32[]{:S(2)}) async-start(f32[8,4,72,128]{3,2,1,0:T(8,128)} %bitcast.40), calls=%async_computation.1 | async-start | bytes 2359296 | tf_op jit(solution)/shard_map/all_to_all | solution.py:179

commit v4 on v3

--- a/solution.py
+++ b/solution.py
@@ -35,89 +35,186 @@
     return shift
 
 
-def cache_kernel(kgrp, live, q_ref, k_ref, v_ref, out_ref,
-                 *, rb, chunk, kv_shift, g_shift, scale):
-    step = pl.program_id(0)
-    rows = q_ref.shape[1]
+def attend_chunks(items, chunk, trips, kv_shift, g_shift, scale):
+    rows = items[0][0].shape[0]
+    head_dim = items[0][0].shape[1]
     width = chunk << kv_shift
     kv_mask = (1 << kv_shift) - 1
     col = lax.broadcasted_iota(jnp.int32, (rows, width), 1)
     row = lax.broadcasted_iota(jnp.int32, (rows, width), 0)
     same_head = (col & kv_mask) == ((row >> g_shift) & kv_mask)
     col_pos = col >> kv_shift
-    lanes = out_ref.shape[2]
-    for slot in range(rb):
-        count = live[step * rb + slot]
-        q = q_ref[slot]
-
-        def body(c, carry):
-            m_prev, l_prev, acc_prev = carry
-            base = pl.multiple_of(c * width, width)
-            keys = k_ref[slot, pl.ds(base, width), :]
-            s = lax.dot_general(q, keys, (((1,), (1,)), ((), ())), preferred_element_type=jnp.float32)
-            s = s * scale
-            valid = same_head & (col_pos + c * chunk < count)
-            s = jnp.where(valid, s, NEG)
-            m_new = jnp.maximum(m_prev, jnp.max(s, axis=1, keepdims=True))
-            alpha = jnp.exp(m_prev - m_new)
-            p = jnp.exp(s - m_new)
-            l_new = alpha * l_prev + jnp.sum(p, axis=1, keepdims=True)
-            acc_new = alpha * acc_prev + jnp.dot(
-                p.astype(jnp.bfloat16), v_ref[slot, pl.ds(base, width), :],
-                preferred_element_type=jnp.float32,
-            )
-            return m_new, l_new, acc_new
-
-        init = (
+
+    def one(c, item, carry):
+        q, kbuf, vbuf, count = item
+        m_prev, l_prev, acc_prev = carry
+        base = pl.multiple_of(c * width, width)
+        keys = kbuf[pl.ds(base, width), :]
+        s = lax.dot_general(q, keys, (((1,), (1,)), ((), ())), preferred_element_type=jnp.float32)
+        s = s * scale
+        valid = same_head & (col_pos + c * chunk < count)
+        s = jnp.where(valid, s, NEG)
+        m_new = jnp.maximum(m_prev, jnp.max(s, axis=1, keepdims=True))
+        alpha = jnp.exp(m_prev - m_new)
+        p = jnp.exp(s - m_new)
+        l_new = alpha * l_prev + jnp.sum(p, axis=1, keepdims=True)
+        acc_new = alpha * acc_prev + jnp.dot(
+            p.astype(jnp.bfloat16), vbuf[pl.ds(base, width), :], preferred_element_type=jnp.float32
+        )
+        return m_new, l_new, acc_new
+
+    def body(c, carries):
+        return tuple(one(c, item, carry) for item, carry in zip(items, carries))
+
+    init = tuple(
+        (
             jnp.full((rows, 1), NEG, jnp.float32),
             jnp.zeros((rows, 1), jnp.float32),
-            jnp.zeros((rows, q_ref.shape[2]), jnp.float32),
+            jnp.zeros((rows, head_dim), jnp.float32),
         )
-        m, l, acc = lax.fori_loop(0, (count + chunk - 1) // chunk, body, init)
-        out_ref[slot, :rows, :] = acc
-        pieces = [jnp.broadcast_to(m, (rows, lanes)), jnp.broadcast_to(l, (rows, lanes))]
-        if lanes > 2 * rows:
-            pieces.append(jnp.zeros((lanes - 2 * rows, lanes), jnp.float32))
-        stacked = jnp.concatenate(pieces, axis=0)
-        out_ref[slot, rows:, :] = jnp.transpose(stacked)[: out_ref.shape[1] - rows, :]
-
-
-def cache_attention(q_blocks, keys, values, live, kv_local, group_size):
+        for _ in items
+    )
+    if isinstance(trips, int) and trips == 1:
+        return body(0, init)
+    return lax.fori_loop(0, trips, body, init)
+
+
+def cache_kernel(live, q_ref, k_hbm, v_hbm, out_ref, kbuf, vbuf, sems,
+                 *, sub, kv_shift, g_shift, scale):
+    reqs, rows, head_dim = q_ref.shape
+    group = kbuf.shape[1]
+    flat_len = kbuf.shape[2]
+    sub_rows = sub << kv_shift
+    subs = flat_len // sub_rows
+    lanes = out_ref.shape[2]
+    local_len = flat_len >> kv_shift
+    vbuf[...] = jnp.zeros(vbuf.shape, vbuf.dtype)
+
+    def copies(first, slot):
+        out = []
+        for member in range(group):
+            for c in range(subs):
+                window = pl.ds(c * sub_rows, sub_rows)
+                out.append((
+                    member,
+                    c,
+                    pltpu.make_async_copy(k_hbm.at[first + member, window, :],
+                                          kbuf.at[slot, member, window, :], sems.at[slot, member, 0, c]),
+                    pltpu.make_async_copy(v_hbm.at[first + member, window, :],
+                                          vbuf.at[slot, member, window, :], sems.at[slot, member, 1, c]),
+                ))
+        return out
+
+    def start(first, slot):
+        for member, c, kc, vc in copies(first, slot):
+            @pl.when(c * sub < live[first + member])
+            def _():
+                kc.start()
+                vc.start()
+
+    def wait(first, slot):
+        for member, c, kc, vc in copies(first, slot):
+            @pl.when(c * sub < live[first + member])
+            def _():
+                kc.wait()
+                vc.wait()
+
+    start(0, 0)
+    small = min(sub, local_len)
+    mid = min(2 * sub, local_len)
+    big = min(4 * sub, local_len)
+
+    def per_group(index, carry):
+        slot = index % 2
+        first = index * group
+
+        @pl.when(first + group < reqs)
+        def _():
+            start(first + group, 1 - slot)
+
+        wait(first, slot)
+        counts = [live[first + member] for member in range(group)]
+        top = counts[0]
+        for count in counts[1:]:
+            top = jnp.maximum(top, count)
+        items = [
+            (q_ref[first + member], kbuf.at[slot, member], vbuf.at[slot, member], counts[member])
+            for member in range(group)
+        ]
+
+        def finish(results):
+            for member, (m, l, acc) in enumerate(results):
+                alive = counts[member] > 0
+                m = jnp.where(alive, m, NEG)
+                l = jnp.where(alive, l, 0.0)
+                acc = jnp.where(alive, acc, 0.0)
+                out_ref[first + member, :rows, :] = acc
+                pieces = [jnp.broadcast_to(m, (rows, lanes)), jnp.broadcast_to(l, (rows, lanes))]
+                if lanes > 2 * rows:
+                    pieces.append(jnp.zeros((lanes - 2 * rows, lanes), jnp.float32))
+                stacked = jnp.concatenate(pieces, axis=0)
+                out_ref[first + member, rows:, :] = jnp.transpose(stacked)[: out_ref.shape[1] - rows, :]
+
+        @pl.when(top == 0)
+        def _():
+            finish([
+                (
+                    jnp.full((rows, 1), NEG, jnp.float32),
+                    jnp.zeros((rows, 1), jnp.float32),
+                    jnp.zeros((rows, head_dim), jnp.float32),
+                )
+                for _ in range(group)
+            ])
+
+        @pl.when((top > 0) & (top <= small))
+        def _():
+            finish(attend_chunks(items, small, 1, kv_shift, g_shift, scale))
+
+        @pl.when((top > small) & (top <= mid))
+        def _():
+            finish(attend_chunks(items, mid, 1, kv_shift, g_shift, scale))
+
+        @pl.when(top > mid)
+        def _():
+            finish(attend_chunks(items, big, (top + big - 1) // big, kv_shift, g_shift, scale))
+
+        return carry
+
+    lax.fori_loop(0, reqs // group, per_group, 0)
+
+
+def cache_attention(q_blocks, keys, values, live, kv_local, group_size, sub=256, group=4):
     reqs, rows, head_dim = q_blocks.shape
     assert 2 * rows <= head_dim
     flat_len = keys.shape[1]
     local_len = flat_len // kv_local
-    chunk = min(256, local_len)
-    rb = 2 if reqs % 2 == 0 else 1
-    steps = reqs // rb
-    step_ids = jnp.arange(steps, dtype=jnp.int32)
-    step_live = jnp.max(live.reshape(steps, rb), axis=1) > 0
-    kgrp = lax.cummax(jnp.where(step_live, step_ids, 0), axis=0)
+    sub = min(sub, local_len)
+    assert local_len % (4 * sub) == 0 or local_len <= 4 * sub
+    group = group if reqs % group == 0 else 1
     kernel = functools.partial(
         cache_kernel,
-        rb=rb,
-        chunk=chunk,
+        sub=sub,
         kv_shift=log2_exact(kv_local),
         g_shift=log2_exact(group_size),
         scale=1.0 / math.sqrt(head_dim),
     )
-    out_rows = rows + 8
-    grid_spec = pltpu.PrefetchScalarGridSpec(
-        num_scalar_prefetch=2,
-        grid=(steps,),
-        in_specs=[
-            pl.BlockSpec((rb, rows, head_dim), lambda i, kg, lv: (i, 0, 0)),
-            pl.BlockSpec((rb, flat_len, head_dim), lambda i, kg, lv: (kg[i], 0, 0)),
-            pl.BlockSpec((rb, flat_len, head_dim), lambda i, kg, lv: (kg[i], 0, 0)),
-        ],
-        out_specs=pl.BlockSpec((rb, out_rows, head_dim), lambda i, kg, lv: (i, 0, 0)),
-    )
+    vmem = pltpu.MemorySpace.VMEM if hasattr(pltpu, "MemorySpace") else pltpu.TPUMemorySpace.VMEM
     return pl.pallas_call(
         kernel,
-        grid_spec=grid_spec,
-        out_shape=jax.ShapeDtypeStruct((reqs, out_rows, head_dim), jnp.float32),
-        compiler_params=pltpu.CompilerParams(dimension_semantics=("arbitrary",)),
-    )(kgrp, live, q_blocks, keys, values)
+        in_specs=[
+            pl.BlockSpec(memory_space=pltpu.SMEM),
+            pl.BlockSpec(memory_space=vmem),
+            pl.BlockSpec(memory_space=pl.ANY),
+            pl.BlockSpec(memory_space=pl.ANY),
+        ],
+        out_specs=pl.BlockSpec(memory_space=vmem),
+        out_shape=jax.ShapeDtypeStruct((reqs, rows + 8, head_dim), jnp.float32),
+        scratch_shapes=[
+            pltpu.VMEM((2, group, flat_len, head_dim), keys.dtype),
+            pltpu.VMEM((2, group, flat_len, head_dim), values.dtype),
+            pltpu.SemaphoreType.DMA((2, group, 2, flat_len // (sub * kv_local))),
+        ],
+    )(live, q_blocks, keys, values)
 
 
 def sum_over(part, axis):

time: 125 us -> 112 us (0.90); the launches traced: 123 us -> 111 us
  Pallas kernels: 34.2 us -> 22.9 us
    pallas_call x1, Pallas kernels: 34.2 us -> 22.9 us  [cache_attention(): pl.pallas_call(kernel, in_specs=[pl.BlockSpec(memory_space=pltpu.SMEM), p...]
where the time goes in v4:
time: 112 us; the launch traced here: 111 us
  waiting for transfers between devices  32.4 us (29%)
  blocking collectives  31.1 us (28%)
  Pallas kernels  22.9 us (20%)
  starting transfers between devices  9.58 us (9%)
  other arithmetic  6.59 us (6%)
  matrix products  6.29 us (6%)
  local copies, waits for them, and re-layouts  2.04 us (2%)
    pallas_call x1, Pallas kernels, cache_attention(): pl.pallas_call(kernel, in_specs=[pl.BlockSpec(memory_space=pltpu.SMEM), p...  22.9 us
    all_to_all x1, waiting for transfers between devices, sum_over(): lax.all_to_all(split, axis, 0, 0).astype(jnp.float32)  17.1 us
    all_to_all x1, waiting for transfers between devices, on_device(): lax.all_to_all(partial.reshape((kv_size, own_reqs) + partial.shape[1:]),...  15.3 us
    all_to_all x1, blocking collectives, sum_over(): lax.all_to_all(split, axis, 0, 0).astype(jnp.float32)  12.3 us
    all_gather x1, blocking collectives, on_device(): lax.all_gather(q_own.reshape(own_reqs, rows_r, head_dim), 'kv', axis=0, t...  9.93 us
    all_gather x1, blocking collectives, on_device(): attended = lax.all_gather(attended, 'kv', axis=0, tiled=True)  8.89 us
    all_to_all x1, starting transfers between devices, sum_over(): lax.all_to_all(split, axis, 0, 0).astype(jnp.float32)  5.3 us
    all_to_all x1, starting transfers between devices, on_device(): lax.all_to_all(partial.reshape((kv_size, own_reqs) + partial.shape[1:]),...  4.27 us
  transfers between devices with their start and end apart: 2, of which 2 were waited for; matrix products, arithmetic and copies ran while one was open for 2% of the time, Pallas kernels for 0%

profile of v4, /device:TPU:0, one launch (start us, length us, event | category | flops | bytes accessed | tf_op | source)
XLA Modules:
  0.0 111.3 jit_solution(6321417056643276428)
XLA Ops:
  0.0 0.0 copy-start
  0.0 1.4 %fusion.17 = f32[128,256]{1,0:T(8,128)S(1)} fusion(bf16[128,640]{1,0:T(8,128)(2,1)} %param.11, bf16[640,256]{1,0:T(8,128)(2,1)} %param.14), kind=kOutput, calls=%fused_computation.50 | convolution fusion | flops 41943040 | bytes 622592 | tf_op jit(solution)/shard_map/dot_general | solution.py:256
  1.4 1.3 %fusion.16 = f32[128,256]{1,0:T(8,128)S(1)} fusion(bf16[128,640]{1,0:T(8,128)(2,1)} %param.11, bf16[640,256]{1,0:T(8,128)(2,1)} %param.13), kind=kOutput, calls=%fused_computation.49 | convolution fusion | flops 41943040 | bytes 622592 | tf_op jit(solution)/shard_map/dot_general | solution.py:255
  2.7 0.6 fusion.15
  3.3 1.2 %pad_maximum_fusion = f32[128,2560]{1,0:T(8,128)} fusion(f32[128,256]{1,0:T(8,128)S(1)} %fusion.17, f32[128,256]{1,0:T(8,128)S(1)} %fusion.16, f32[128,2048]{1,0:T(8,128)S(1)} %fusion.15), kind=kLoop, calls=%fused_computation | loop fusion | flops 655360 | bytes 2621440 | tf_op jit(solution)/shard_map/concatenate | solution.py:252
  4.5 5.3 %all-to-all-start = ((f32[8,16,2560]{2,1,0:T(8,128)}), f32[8,16,2560]{2,1,0:T(8,128)}, u32[]{:S(2)}, u32[]{:S(2)}) async-start(f32[8,16,2560]{2,1,0:T(8,128)} %bitcast.37), calls=%async_computation | async-start | bytes 2621440 | tf_op jit(solution)/shard_map/all_to_all | solution.py:223
  9.8 0.0 copy-done.4
  9.8 0.1 copy.45
  9.9 0.1 reshape.202
  10.0 0.1 constant_dynamic-slice_fusion
  10.1 0.1 copy.47
  10.2 0.1 dynamic-slice_convert_fusion
  10.3 0.0 copy-done.6
  10.3 0.5 subtract_clamp_fusion.live
  10.8 0.1 and_or_fusion
  10.9 0.1 multiply_cosine_fusion
  11.0 17.1 %all-to-all-done = f32[8,16,2560]{2,1,0:T(8,128)} async-done(((f32[8,16,2560]{2,1,0:T(8,128)}), f32[8,16,2560]{2,1,0:T(8,128)}, u32[]{:S(2)}, u32[]{:S(2)}) %all-to-all-start) | async-done | bytes 1310752 | tf_op jit(solution)/shard_map/all_to_all | solution.py:223
  28.1 1.4 %reduce_sum.68 = f32[16,2560]{1,0:T(8,128)S(1)} reduce(f32[8,16,2560]{2,1,0:T(8,128)} %all-to-all-done, f32[]{:T(128)} %constant.9.clone.1), dimensions={0}, to_apply=%region_0.0 | reduce | flops 286720 | bytes 1474564 | tf_op jit(solution)/shard_map/reduce_sum | solution.py:223
  29.6 0.1 multiply_reduce_fusion
  29.7 0.0 copy-done.3
  29.7 0.1 multiply_multiply_fusion
  29.8 0.1 multiply_subtract_fusion
  30.0 0.1 maximum_convert_fusion
  30.1 9.9 %all_gather.6.q_ref = bf16[32,64,128]{2,1,0:T(8,128)(2,1)} all-gather(bf16[4,64,128]{2,1,0:T(8,128)(2,1)S(1)} %bitcast.41), channel_id=1, replica_groups=mesh['kv'=8,'head'=4] {'kv'}, dimensions={0}, use_global_device_ids=true | all-gather | bytes 589824 | tf_op jit(solution)/shard_map/all_gather | solution.py:266
  40.0 22.9 %shard_map.109 = f32[32,72,128]{2,1,0:T(8,128)} custom-call(s32[32]{0:T(128)} %subtract_clamp_fusion.live, bf16[32,64,128]{2,1,0:T(8,128)(2,1)} %all_gather.6.q_ref, bf16[32,2048,128]{2,1,0:T(8,128)(2,1)} %bitcast.35, bf16[32,2048,128]{2,1,0:T(8,128)(2,1)} %bitcast.36), custom_call_target="tpu_custom_call" | custom-call | tf_op jit(solution)/shard_map/pallas_call | solution.py:202
  62.9 0.0 copy-done.2
  62.9 0.0 copy-start.5
  63.0 0.0 slice-start
  63.0 4.3 %all-to-all-start.1 = ((f32[8,4,72,128]{3,2,1,0:T(8,128)}), f32[8,4,72,128]{3,2,1,0:T(8,128)}, u32[]{:S(2)}, u32[]{:S(2)}) async-start(f32[8,4,72,128]{3,2,1,0:T(8,128)} %bitcast.38), calls=%async_computation.1 | async-start | bytes 2359296 | tf_op jit(solution)/shard_map/all_to_all | solution.py:276
  67.3 0.1 multiply_reduce_fusion.2
  67.4 0.0 copy-done.5
  67.4 0.1 multiply_multiply_fusion.1
  67.5 0.1 subtract_convert_fusion
  67.6 0.1 pad_maximum_fusion.1
  67.7 0.4 fusion.14
  68.1 0.1 reshape.207
  68.2 0.1 fusion.4
  68.3 0.1 reshape.210
  68.4 0.3 convolution_bitcast_fusion
  68.8 15.3 %all-to-all-done.1 = f32[8,4,72,128]{3,2,1,0:T(8,128)} async-done(((f32[8,4,72,128]{3,2,1,0:T(8,128)}), f32[8,4,72,128]{3,2,1,0:T(8,128)}, u32[]{:S(2)}, u32[]{:S(2)}) %all-to-all-start.1) | async-done | bytes 1179680 | tf_op jit(solution)/shard_map/all_to_all | solution.py:276
  84.1 1.1 fusion.13
  85.2 0.1 div.35
  85.4 1.6 %fusion.2 = f32[4,64,128]{2,1,0:T(8,128)S(1)} fusion(f32[8,4,72,128]{3,2,1,0:T(8,128)} %all-to-all-done.1, f32[8,4,64]{2,1,0:T(4,128)S(1)} %get-tuple-element.8), kind=kLoop, calls=%fused_computation.7 | loop fusion | flops 491520 | bytes 1187840 | tf_op jit(solution)/shard_map/reduce_sum | solution.py:307
  87.0 0.1 mul.205
  87.1 8.9 %all_gather.7 = bf16[128,2048]{1,0:T(8,128)(2,1)S(1)} all-gather(bf16[16,2048]{1,0:T(8,128)(2,1)S(1)} %divide_convert_fusion), channel_id=1, replica_groups=mesh['kv'=8,'head'=4] {'kv'}, dimensions={0}, use_global_device_ids=true | all-gather | bytes 589824 | tf_op jit(solution)/shard_map/all_gather | solution.py:309
  96.0 2.3 %convolution_convert_fusion = bf16[128,640]{1,0:T(8,128)(2,1)S(1)} fusion(bf16[128,2048]{1,0:T(8,128)(2,1)S(1)} %all_gather.7, bf16[2048,640]{1,0:T(8,128)(2,1)} %param.21), kind=kOutput, calls=%fused_computation.1 | convolution fusion | flops 335626240 | bytes 3309568 | tf_op jit(solution)/shard_map/dot_general | solution.py:310
  98.4 12.3 %all_to_all.15 = bf16[4,32,640]{2,1,0:T(8,128)(2,1)S(1)} all-to-all(bf16[4,32,640]{2,1,0:T(8,128)(2,1)S(1)} %bitcast.40), channel_id=1, replica_groups=mesh['kv'=8,'head'=4] {'head'}, dimensions={0} | all-to-all | bytes 327680 | tf_op jit(solution)/shard_map/all_to_all | solution.py:223
  110.7 0.6 reduce_sum.75
  (29 shorter events, 0.4 us)
Async XLA Ops:
  0.0 2.7 %copy-start = (bf16[640,2048]{1,0:T(8,128)(2,1)S(1)}, bf16[640,2048]{1,0:T(8,128)(2,1)}, u32[]{:S(2)}) copy-start(bf16[640,2048]{1,0:T(8,128)(2,1)} %param.12) | copy-start | bytes 7864324
  0.0 2.7 %copy-start.1 = (bf16[128,640]{1,0:T(8,128)(2,1)S(1)}, bf16[128,640]{1,0:T(8,128)(2,1)}, u32[]{:S(2)}) copy-start(bf16[128,640]{1,0:T(8,128)(2,1)} %param.11) | copy-start | bytes 491524
  4.5 5.3 %copy-start.4 = (s32[32,4]{0,1:T(4,128)S(1)}, s32[32,4]{0,1:T(4,128)}, u32[]{:S(2)}) copy-start(s32[32,4]{0,1:T(4,128)} %param.20) | copy-start | bytes 1540
  4.5 5.8 %copy-start.6 = (s32[32]{0:T(128)S(1)}, s32[32]{0:T(128)}, u32[]{:S(2)}) copy-start(s32[32]{0:T(128)} %param.19) | copy-start | bytes 388
  4.5 23.6 %all-to-all-start = ((f32[8,16,2560]{2,1,0:T(8,128)}), f32[8,16,2560]{2,1,0:T(8,128)}, u32[]{:S(2)}, u32[]{:S(2)}) async-start(f32[8,16,2560]{2,1,0:T(8,128)} %bitcast.37), calls=%async_computation | async-start | bytes 2621440 | tf_op jit(solution)/shard_map/all_to_all | solution.py:223
  9.8 19.9 %copy-start.3 = (f32[16,128]{1,0:T(8,128)S(1)}, f32[16,128]{1,0:T(8,128)}, u32[]{:S(2)}) copy-start(f32[16,128]{1,0:T(8,128)} %param.15) | copy-start | bytes 24580
  29.5 33.4 %copy-start.2 = (f32[16,2560]{1,0:T(8,128)}, f32[16,2560]{1,0:T(8,128)S(1)}, u32[]{:S(2)}) copy-start(f32[16,2560]{1,0:T(8,128)S(1)} %reduce_sum.68) | copy-start | bytes 491524
  62.9 4.4 %copy-start.5 = (f32[2,128]{1,0:T(2,128)S(1)}, f32[2,128]{1,0:T(2,128)}, u32[]{:S(2)}) copy-start(f32[2,128]{1,0:T(2,128)} %param.16) | copy-start | bytes 3076
  63.0 4.3 %slice-start = ((f32[16,2560]{1,0:T(8,128)}), f32[16,256]{1,0:T(8,128)S(1)}, s32[]{:S(2)}) async-start(f32[16,2560]{1,0:T(8,128)} %copy-done.2), calls=%async_computation.3 | async-start | bytes 32768 | tf_op jit(solution)/shard_map/slice | solution.py:263
  63.0 21.1 %all-to-all-start.1 = ((f32[8,4,72,128]{3,2,1,0:T(8,128)}), f32[8,4,72,128]{3,2,1,0:T(8,128)}, u32[]{:S(2)}, u32[]{:S(2)}) async-start(f32[8,4,72,128]{3,2,1,0:T(8,128)} %bitcast.38), calls=%async_computation.1 | async-start | bytes 2359296 | tf_op jit(solution)/shard_map/all_to_all | solution.py:276

commit v5 on v4

--- a/solution.py
+++ b/solution.py
@@ -33,6 +33,20 @@
     shift = value.bit_length() - 1
     assert (1 << shift) == value
     return shift
+
+
+def split_pieces(value, count):
+    pieces = []
+    rest = value
+    for _ in range(count):
+        piece = rest.astype(jnp.bfloat16).astype(jnp.float32)
+        pieces.append(piece)
+        rest = rest - piece
+    return pieces
+
+
+def stat_groups(vectors, per_row):
+    return [vectors[i:i + per_row] for i in range(0, len(vectors), per_row)]
 
 
 def attend_chunks(items, chunk, trips, kv_shift, g_shift, scale):
@@ -147,13 +161,15 @@
                 alive = counts[member] > 0
                 m = jnp.where(alive, m, NEG)
                 l = jnp.where(alive, l, 0.0)
-                acc = jnp.where(alive, acc, 0.0)
-                out_ref[first + member, :rows, :] = acc
-                pieces = [jnp.broadcast_to(m, (rows, lanes)), jnp.broadcast_to(l, (rows, lanes))]
-                if lanes > 2 * rows:
-                    pieces.append(jnp.zeros((lanes - 2 * rows, lanes), jnp.float32))
-                stacked = jnp.concatenate(pieces, axis=0)
-                out_ref[first + member, rows:, :] = jnp.transpose(stacked)[: out_ref.shape[1] - rows, :]
+                acc = jnp.where(alive, acc / jnp.where(alive, l, 1.0), 0.0)
+                out_ref[first + member, :rows, :] = acc.astype(out_ref.dtype)
+                stat_rows = [jnp.zeros((1, lanes), jnp.float32)] * (out_ref.shape[1] - rows)
+                for at, piece_group in enumerate(stat_groups(split_pieces(m, 3) + split_pieces(l, 2), lanes // rows)):
+                    pieces = [jnp.broadcast_to(v, (rows, lanes)) for v in piece_group]
+                    if lanes > rows * len(piece_group):
+                        pieces.append(jnp.zeros((lanes - rows * len(piece_group), lanes), jnp.float32))
+                    stat_rows[at] = jnp.transpose(jnp.concatenate(pieces, axis=0))[:1, :]
+                out_ref[first + member, rows:, :] = jnp.concatenate(stat_rows, axis=0).astype(out_ref.dtype)
 
         @pl.when(top == 0)
         def _():
@@ -208,7 +224,7 @@
             pl.BlockSpec(memory_space=pl.ANY),
         ],
         out_specs=pl.BlockSpec(memory_space=vmem),
-        out_shape=jax.ShapeDtypeStruct((reqs, rows + 8, head_dim), jnp.float32),
+        out_shape=jax.ShapeDtypeStruct((reqs, rows + 16, head_dim), jnp.bfloat16),
         scratch_shapes=[
             pltpu.VMEM((2, group, flat_len, head_dim), keys.dtype),
             pltpu.VMEM((2, group, flat_len, head_dim), values.dtype),
@@ -257,7 +273,7 @@
         ],
         axis=1,
     )
-    proj_own = sum_over(proj, "kv")
+    proj_own = sum_over(proj.astype(jnp.bfloat16), "kv")
     pos_own = lax.dynamic_slice_in_dim(positions.reshape(rows), row0, own_rows)
     q_own = norm_rotate(proj_own[:, :q_width], q_gain, pos_own)
     k_own = norm_rotate(proj_own[:, q_width:q_width + k_width], key_norm_scale, pos_own)
@@ -276,9 +292,16 @@
     gathered = lax.all_to_all(
         partial.reshape((kv_size, own_reqs) + partial.shape[1:]), "kv", 0, 0
     )
-    acc_g = gathered[:, :, :rows_r, :]
-    m_g = gathered[:, :, rows_r, :rows_r]
-    l_g = gathered[:, :, rows_r, rows_r:2 * rows_r]
+    acc_g = gathered[:, :, :rows_r, :].astype(jnp.float32)
+    per_row = head_dim // rows_r
+    stats = gathered[:, :, rows_r:, :].astype(jnp.float32)
+
+    def stat(k):
+        lane0 = (k % per_row) * rows_r
+        return stats[:, :, k // per_row, lane0:lane0 + rows_r]
+
+    m_g = stat(0) + stat(1) + stat(2)
+    l_g = stat(3) + stat(4)
 
     scale = 1.0 / math.sqrt(head_dim)
     q_d = q_own.reshape(own_reqs, drafts, kv_local, group_size, head_dim)
@@ -301,9 +324,9 @@
     m_d = m_d.reshape(own_reqs, rows_r)
 
     top = jnp.maximum(jnp.max(m_g, axis=0), m_d)
-    ratio = jnp.exp(m_g - top[None])
+    ratio = jnp.exp(m_g - top[None]) * l_g
     ratio_d = jnp.exp(m_d - top)
-    total = jnp.sum(l_g * ratio, axis=0) + l_d * ratio_d
+    total = jnp.sum(ratio, axis=0) + l_d * ratio_d
     acc = jnp.sum(acc_g * ratio[..., None], axis=0) + acc_d * ratio_d[..., None]
     attended = (acc / total[..., None]).astype(jnp.bfloat16).reshape(own_rows, q_width)
     attended = lax.all_gather(attended, "kv", axis=0, tiled=True)

time: 112 us -> 95.8 us (0.86)
  waiting for transfers between devices: 32.4 us -> 19.8 us
  other arithmetic: 6.59 us -> 3.9 us
    all_to_all x1, waiting for transfers between devices: 17.1 us -> 9.96 us  [sum_over(): lax.all_to_all(split, axis, 0, 0).astype(jnp.float32)]
    all_to_all x1, waiting for transfers between devices: 15.3 us -> 9.88 us  [on_device(): lax.all_to_all(partial.reshape((kv_size, own_reqs) + partial.shape[1:]),...]
    reduce_sum x2, other arithmetic: 2.04 us -> 0.73 us  [sum_over(): jnp.sum(lax.all_to_all(split, axis, 0, 0).astype(jnp.float32), axis=0)]
    reduce_sum x1, other arithmetic: 1.58 us -> 0.34 us  [on_device(): acc = jnp.sum(acc_g * ratio[..., None], axis=0) + acc_d * ratio_d[..., None]]
where the time goes in v5:
time: 95.8 us; the launch traced here: 94.9 us
  blocking collectives  30.7 us (32%)
  Pallas kernels  23.2 us (24%)
  waiting for transfers between devices  19.8 us (21%)
  starting transfers between devices  8.72 us (9%)
  matrix products  7.22 us (8%)
  other arithmetic  3.9 us (4%)
  local copies, waits for them, and re-layouts  0.96 us (1%)
    pallas_call x1, Pallas kernels, cache_attention(): pl.pallas_call(kernel, in_specs=[pl.BlockSpec(memory_space=pltpu.SMEM), p...  23.2 us
    all_to_all x1, blocking collectives, sum_over(): lax.all_to_all(split, axis, 0, 0).astype(jnp.float32)  11.9 us
    all_to_all x1, waiting for transfers between devices, sum_over(): lax.all_to_all(split, axis, 0, 0).astype(jnp.float32)  9.96 us
    all_gather x1, blocking collectives, on_device(): lax.all_gather(q_own.reshape(own_reqs, rows_r, head_dim), 'kv', axis=0, t...  9.93 us
    all_to_all x1, waiting for transfers between devices, on_device(): lax.all_to_all(partial.reshape((kv_size, own_reqs) + partial.shape[1:]),...  9.88 us
    all_gather x1, blocking collectives, on_device(): attended = lax.all_gather(attended, 'kv', axis=0, tiled=True)  8.9 us
    all_to_all x1, starting transfers between devices, sum_over(): lax.all_to_all(split, axis, 0, 0).astype(jnp.float32)  5.17 us
    all_to_all x1, starting transfers between devices, on_device(): lax.all_to_all(partial.reshape((kv_size, own_reqs) + partial.shape[1:]),...  3.55 us
  transfers between devices with their start and end apart: 2, of which 2 were waited for; matrix products, arithmetic and copies ran while one was open for 2% of the time, Pallas kernels for 0%

profile of v5, /device:TPU:0, one launch (start us, length us, event | category | flops | bytes accessed | tf_op | source)
XLA Modules:
  0.0 94.9 jit_solution(13111445286136489923)
XLA Ops:
  0.0 0.0 copy-start
  0.0 1.4 %convolution_convert_fusion.3 = bf16[128,256]{1,0:T(8,128)(2,1)S(1)} fusion(bf16[128,640]{1,0:T(8,128)(2,1)} %param.11, bf16[640,256]{1,0:T(8,128)(2,1)} %param.13), kind=kOutput, calls=%fused_computation.5 | convolution fusion | flops 41975808 | bytes 557056 | tf_op jit(solution)/shard_map/dot_general | solution.py:271
  1.4 1.3 %convolution_convert_fusion.2 = bf16[128,256]{1,0:T(8,128)(2,1)S(1)} fusion(bf16[128,640]{1,0:T(8,128)(2,1)} %param.11, bf16[640,256]{1,0:T(8,128)(2,1)} %param.14), kind=kOutput, calls=%fused_computation.4 | convolution fusion | flops 41975808 | bytes 557056 | tf_op jit(solution)/shard_map/dot_general | solution.py:272
  2.7 0.0 copy-done
  2.7 0.0 copy-start.2
  2.7 0.0 copy-start.4
  2.7 1.5 %convolution_convert_fusion = bf16[128,2048]{1,0:T(8,128)(2,1)S(1)} fusion(bf16[128,640]{1,0:T(8,128)(2,1)} %param.11, bf16[640,2048]{1,0:T(8,128)(2,1)S(1)} %copy-done), kind=kOutput, calls=%fused_computation | convolution fusion | flops 335806464 | bytes 3309568 | tf_op jit(solution)/shard_map/dot_general | solution.py:270
  4.2 0.0 copy-start.1
  4.3 0.0 copy-start.3
  4.3 0.9 pad_maximum_fusion
  5.2 5.2 %all-to-all-start = ((bf16[8,16,2560]{2,1,0:T(8,128)(2,1)}), bf16[8,16,2560]{2,1,0:T(8,128)(2,1)S(1)}, u32[]{:S(2)}, u32[]{:S(2)}) async-start(bf16[8,16,2560]{2,1,0:T(8,128)(2,1)} %pad_maximum_fusion), calls=%async_computation | async-start | bytes 1310720 | tf_op jit(solution)/shard_map/all_to_all | solution.py:239
  10.4 0.1 copy.53
  10.4 0.1 constant_dynamic-slice_fusion
  10.5 0.1 reshape.228
  10.6 0.0 copy-done.4
  10.6 0.5 subtract_clamp_fusion.live
  11.1 0.1 dynamic-slice_convert_fusion
  11.2 0.1 copy.57
  11.3 0.1 and_or_fusion
  11.4 0.1 multiply_cosine_fusion
  11.5 10.0 %all-to-all-done = bf16[8,16,2560]{2,1,0:T(8,128)(2,1)S(1)} async-done(((bf16[8,16,2560]{2,1,0:T(8,128)(2,1)}), bf16[8,16,2560]{2,1,0:T(8,128)(2,1)S(1)}, u32[]{:S(2)}, u32[]{:S(2)}) %all-to-all-start) | async-done | bytes 655392 | tf_op jit(solution)/shard_map/all_to_all | solution.py:239
  21.5 0.1 convert_reduce_fusion
  21.7 0.1 multiply_reduce_fusion.1
  21.8 0.1 multiply_reduce_fusion.2
  21.9 0.0 copy-done.1
  21.9 0.1 multiply_multiply_fusion
  22.0 0.1 multiply_multiply_fusion.1
  22.1 0.1 multiply_subtract_fusion
  22.2 0.1 subtract_convert_fusion
  22.3 0.1 maximum_convert_fusion
  22.4 9.9 %all_gather.6.q_ref = bf16[32,64,128]{2,1,0:T(8,128)(2,1)} all-gather(bf16[4,64,128]{2,1,0:T(8,128)(2,1)S(1)} %bitcast.50), channel_id=1, replica_groups=mesh['kv'=8,'head'=4] {'kv'}, dimensions={0}, use_global_device_ids=true | all-gather | bytes 589824 | tf_op jit(solution)/shard_map/all_gather | solution.py:282
  32.4 23.2 %shard_map.109 = bf16[32,80,128]{2,1,0:T(8,128)(2,1)} custom-call(s32[32]{0:T(128)} %subtract_clamp_fusion.live, bf16[32,64,128]{2,1,0:T(8,128)(2,1)} %all_gather.6.q_ref, bf16[32,2048,128]{2,1,0:T(8,128)(2,1)} %bitcast.44, bf16[32,2048,128]{2,1,0:T(8,128)(2,1)} %bitcast.45), custom_call_target="tpu_custom_call" | custom-call | tf_op jit(solution)/shard_map/pallas_call | solution.py:218
  55.6 3.6 %all-to-all-start.1 = ((bf16[8,4,80,128]{3,2,1,0:T(8,128)(2,1)}), bf16[8,4,80,128]{3,2,1,0:T(8,128)(2,1)S(1)}, u32[]{:S(2)}, u32[]{:S(2)}) async-start(bf16[8,4,80,128]{3,2,1,0:T(8,128)(2,1)} %bitcast.46), calls=%async_computation.1 | async-start | bytes 1310720 | tf_op jit(solution)/shard_map/all_to_all | solution.py:292
  59.1 0.1 pad_maximum_fusion.1
  59.2 0.4 fusion.18
  59.7 0.1 fusion.3
  59.8 0.1 reshape.236
  59.9 0.1 reshape.233
  60.0 0.3 convolution_bitcast_fusion
  60.3 9.9 %all-to-all-done.1 = bf16[8,4,80,128]{3,2,1,0:T(8,128)(2,1)S(1)} async-done(((bf16[8,4,80,128]{3,2,1,0:T(8,128)(2,1)}), bf16[8,4,80,128]{3,2,1,0:T(8,128)(2,1)S(1)}, u32[]{:S(2)}, u32[]{:S(2)}) %all-to-all-start.1) | async-done | bytes 655392 | tf_op jit(solution)/shard_map/all_to_all | solution.py:292
  70.2 0.1 fusion.17
  70.4 0.3 multiply_reduce_fusion
  70.8 0.1 div.35
  71.0 0.1 mul.210
  71.1 8.9 %all_gather.7 = bf16[128,2048]{1,0:T(8,128)(2,1)S(1)} all-gather(bf16[16,2048]{1,0:T(8,128)(2,1)S(1)} %divide_convert_fusion), channel_id=1, replica_groups=mesh['kv'=8,'head'=4] {'kv'}, dimensions={0}, use_global_device_ids=true | all-gather | bytes 589824 | tf_op jit(solution)/shard_map/all_gather | solution.py:332
  80.0 2.3 %convolution_convert_fusion.1 = bf16[128,640]{1,0:T(8,128)(2,1)S(1)} fusion(bf16[128,2048]{1,0:T(8,128)(2,1)S(1)} %all_gather.7, bf16[2048,640]{1,0:T(8,128)(2,1)} %param.21), kind=kOutput, calls=%fused_computation.2 | convolution fusion | flops 335626240 | bytes 3309568 | tf_op jit(solution)/shard_map/dot_general | solution.py:333
  82.4 11.9 %all_to_all.15 = bf16[4,32,640]{2,1,0:T(8,128)(2,1)S(1)} all-to-all(bf16[4,32,640]{2,1,0:T(8,128)(2,1)S(1)} %bitcast.49), channel_id=1, replica_groups=mesh['kv'=8,'head'=4] {'head'}, dimensions={0} | all-to-all | bytes 327680 | tf_op jit(solution)/shard_map/all_to_all | solution.py:239
  94.3 0.6 reduce_sum.75
  (25 shorter events, 0.4 us)
Async XLA Ops:
  0.0 2.7 %copy-start = (bf16[640,2048]{1,0:T(8,128)(2,1)S(1)}, bf16[640,2048]{1,0:T(8,128)(2,1)}, u32[]{:S(2)}) copy-start(bf16[640,2048]{1,0:T(8,128)(2,1)} %param.12) | copy-start | bytes 7864324
  2.7 7.6 %copy-start.2 = (s32[32,4]{0,1:T(4,128)S(1)}, s32[32,4]{0,1:T(4,128)}, u32[]{:S(2)}) copy-start(s32[32,4]{0,1:T(4,128)} %param.20) | copy-start | bytes 1540
  2.7 7.9 %copy-start.4 = (s32[32]{0:T(128)S(1)}, s32[32]{0:T(128)}, u32[]{:S(2)}) copy-start(s32[32]{0:T(128)} %param.19) | copy-start | bytes 388
  4.2 17.7 %copy-start.1 = (f32[16,128]{1,0:T(8,128)S(1)}, f32[16,128]{1,0:T(8,128)}, u32[]{:S(2)}) copy-start(f32[16,128]{1,0:T(8,128)} %param.15) | copy-start | bytes 24580
  4.3 17.8 %copy-start.3 = (f32[2,128]{1,0:T(2,128)S(1)}, f32[2,128]{1,0:T(2,128)}, u32[]{:S(2)}) copy-start(f32[2,128]{1,0:T(2,128)} %param.16) | copy-start | bytes 3076
  5.2 16.3 %all-to-all-start = ((bf16[8,16,2560]{2,1,0:T(8,128)(2,1)}), bf16[8,16,2560]{2,1,0:T(8,128)(2,1)S(1)}, u32[]{:S(2)}, u32[]{:S(2)}) async-start(bf16[8,16,2560]{2,1,0:T(8,128)(2,1)} %pad_maximum_fusion), calls=%async_computation | async-start | bytes 1310720 | tf_op jit(solution)/shard_map/all_to_all | solution.py:239
  55.6 14.6 %all-to-all-start.1 = ((bf16[8,4,80,128]{3,2,1,0:T(8,128)(2,1)}), bf16[8,4,80,128]{3,2,1,0:T(8,128)(2,1)S(1)}, u32[]{:S(2)}, u32[]{:S(2)}) async-start(bf16[8,4,80,128]{3,2,1,0:T(8,128)(2,1)} %bitcast.46), calls=%async_computation.1 | async-start | bytes 1310720 | tf_op jit(solution)/shard_map/all_to_all | solution.py:292

commit v6 on v5

--- a/solution.py
+++ b/solution.py
@@ -93,7 +93,7 @@
     return lax.fori_loop(0, trips, body, init)
 
 
-def cache_kernel(live, q_ref, k_hbm, v_hbm, out_ref, kbuf, vbuf, sems,
+def cache_kernel(order, live, q_ref, k_hbm, v_hbm, out_ref, kbuf, vbuf, sems,
                  *, sub, kv_shift, g_shift, scale):
     reqs, rows, head_dim = q_ref.shape
     group = kbuf.shape[1]
@@ -102,41 +102,51 @@
     subs = flat_len // sub_rows
     lanes = out_ref.shape[2]
     local_len = flat_len >> kv_shift
-    vbuf[...] = jnp.zeros(vbuf.shape, vbuf.dtype)
+
+    small = min(sub, local_len)
+    mid = min(2 * sub, local_len)
+    big = min(4 * sub, local_len)
+
+    def group_of(first):
+        members = [order[first + member] for member in range(group)]
+        counts = [live[req] for req in members]
+        top = counts[0]
+        for count in counts[1:]:
+            top = jnp.maximum(top, count)
+        span = jnp.where(top <= small, small, jnp.where(top <= mid, mid, ((top + big - 1) // big) * big))
+        span = jnp.where(top > 0, span, 0)
+        return members, counts, top, span
 
     def copies(first, slot):
+        members, _, _, span = group_of(first)
         out = []
         for member in range(group):
             for c in range(subs):
                 window = pl.ds(c * sub_rows, sub_rows)
                 out.append((
-                    member,
-                    c,
-                    pltpu.make_async_copy(k_hbm.at[first + member, window, :],
+                    c * sub < span,
+                    pltpu.make_async_copy(k_hbm.at[members[member], window, :],
                                           kbuf.at[slot, member, window, :], sems.at[slot, member, 0, c]),
-                    pltpu.make_async_copy(v_hbm.at[first + member, window, :],
+                    pltpu.make_async_copy(v_hbm.at[members[member], window, :],
                                           vbuf.at[slot, member, window, :], sems.at[slot, member, 1, c]),
                 ))
         return out
 
     def start(first, slot):
-        for member, c, kc, vc in copies(first, slot):
-            @pl.when(c * sub < live[first + member])
+        for needed, kc, vc in copies(first, slot):
+            @pl.when(needed)
             def _():
                 kc.start()
                 vc.start()
 
     def wait(first, slot):
-        for member, c, kc, vc in copies(first, slot):
-            @pl.when(c * sub < live[first + member])
+        for needed, kc, vc in copies(first, slot):
+            @pl.when(needed)
             def _():
                 kc.wait()
                 vc.wait()
 
     start(0, 0)
-    small = min(sub, local_len)
-    mid = min(2 * sub, local_len)
-    big = min(4 * sub, local_len)
 
     def per_group(index, carry):
         slot = index % 2
@@ -147,12 +157,9 @@
             start(first + group, 1 - slot)
 
         wait(first, slot)
-        counts = [live[first + member] for member in range(group)]
-        top = counts[0]
-        for count in counts[1:]:
-            top = jnp.maximum(top, count)
+        members, counts, top, _ = group_of(first)
         items = [
-            (q_ref[first + member], kbuf.at[slot, member], vbuf.at[slot, member], counts[member])
+            (q_ref[members[member]], kbuf.at[slot, member], vbuf.at[slot, member], counts[member])
             for member in range(group)
         ]
 
@@ -162,14 +169,14 @@
                 m = jnp.where(alive, m, NEG)
                 l = jnp.where(alive, l, 0.0)
                 acc = jnp.where(alive, acc / jnp.where(alive, l, 1.0), 0.0)
-                out_ref[first + member, :rows, :] = acc.astype(out_ref.dtype)
+                out_ref[members[member], :rows, :] = acc.astype(out_ref.dtype)
                 stat_rows = [jnp.zeros((1, lanes), jnp.float32)] * (out_ref.shape[1] - rows)
                 for at, piece_group in enumerate(stat_groups(split_pieces(m, 3) + split_pieces(l, 2), lanes // rows)):
                     pieces = [jnp.broadcast_to(v, (rows, lanes)) for v in piece_group]
                     if lanes > rows * len(piece_group):
                         pieces.append(jnp.zeros((lanes - rows * len(piece_group), lanes), jnp.float32))
                     stat_rows[at] = jnp.transpose(jnp.concatenate(pieces, axis=0))[:1, :]
-                out_ref[first + member, rows:, :] = jnp.concatenate(stat_rows, axis=0).astype(out_ref.dtype)
+                out_ref[members[member], rows:, :] = jnp.concatenate(stat_rows, axis=0).astype(out_ref.dtype)
 
         @pl.when(top == 0)
         def _():
@@ -214,10 +221,15 @@
         g_shift=log2_exact(group_size),
         scale=1.0 / math.sqrt(head_dim),
     )
+    ids = jnp.arange(reqs, dtype=jnp.int32)
+    sort_key = live * reqs + ids
+    rank = jnp.sum((sort_key[None, :] < sort_key[:, None]).astype(jnp.int32), axis=1)
+    order = jnp.sum(jnp.where(rank[None, :] == ids[:, None], ids[None, :], 0), axis=1).astype(jnp.int32)
     vmem = pltpu.MemorySpace.VMEM if hasattr(pltpu, "MemorySpace") else pltpu.TPUMemorySpace.VMEM
     return pl.pallas_call(
         kernel,
         in_specs=[
+            pl.BlockSpec(memory_space=pltpu.SMEM),
             pl.BlockSpec(memory_space=pltpu.SMEM),
             pl.BlockSpec(memory_space=vmem),
             pl.BlockSpec(memory_space=pl.ANY),
@@ -230,7 +242,7 @@
             pltpu.VMEM((2, group, flat_len, head_dim), values.dtype),
             pltpu.SemaphoreType.DMA((2, group, 2, flat_len // (sub * kv_local))),
         ],
-    )(live, q_blocks, keys, values)
+    )(order, live, q_blocks, keys, values)
 
 
 def sum_over(part, axis):

time: 95.8 us -> 90.5 us (0.945)
  Pallas kernels: 23.2 us -> 18.3 us
    pallas_call x1, Pallas kernels: 23.2 us -> 18.3 us  [cache_attention(): pl.pallas_call(kernel, in_specs=[pl.BlockSpec(memory_space=pltpu.SMEM), p...]
  transfers between devices with their start and end apart: 2 -> 2, of which waited for: 2 -> 2; matrix products, arithmetic and copies ran while one was open for 2% -> 4% of each run, Pallas kernels for 0% -> 0%
where the time goes in v6:
time: 90.5 us; the launch traced here: 90 us
  blocking collectives  30.7 us (34%)
  waiting for transfers between devices  19 us (21%)
  Pallas kernels  18.3 us (20%)
  starting transfers between devices  8.72 us (10%)
  matrix products  7.22 us (8%)
  other arithmetic  4.77 us (5%)
  local copies, waits for them, and re-layouts  0.96 us (1%)
    pallas_call x1, Pallas kernels, cache_attention(): pl.pallas_call(kernel, in_specs=[pl.BlockSpec(memory_space=pltpu.SMEM), p...  18.3 us
    all_to_all x1, blocking collectives, sum_over(): lax.all_to_all(split, axis, 0, 0).astype(jnp.float32)  11.9 us
    all_gather x1, blocking collectives, on_device(): lax.all_gather(q_own.reshape(own_reqs, rows_r, head_dim), 'kv', axis=0, t...  9.93 us
    all_to_all x1, waiting for transfers between devices, on_device(): lax.all_to_all(partial.reshape((kv_size, own_reqs) + partial.shape[1:]),...  9.88 us
    all_to_all x1, waiting for transfers between devices, sum_over(): lax.all_to_all(split, axis, 0, 0).astype(jnp.float32)  9.09 us
    all_gather x1, blocking collectives, on_device(): attended = lax.all_gather(attended, 'kv', axis=0, tiled=True)  8.9 us
    all_to_all x1, starting transfers between devices, sum_over(): lax.all_to_all(split, axis, 0, 0).astype(jnp.float32)  5.17 us
    all_to_all x1, starting transfers between devices, on_device(): lax.all_to_all(partial.reshape((kv_size, own_reqs) + partial.shape[1:]),...  3.55 us
  transfers between devices with their start and end apart: 2, of which 2 were waited for; matrix products, arithmetic and copies ran while one was open for 4% of the time, Pallas kernels for 0%

profile of v6, /device:TPU:0, one launch (start us, length us, event | category | flops | bytes accessed | tf_op | source)
XLA Modules:
  0.0 90.0 jit_solution(6723276381847200953)
XLA Ops:
  0.0 0.0 copy-start
  0.0 1.4 %convolution_convert_fusion.3 = bf16[128,256]{1,0:T(8,128)(2,1)S(1)} fusion(bf16[128,640]{1,0:T(8,128)(2,1)} %param.11, bf16[640,256]{1,0:T(8,128)(2,1)} %param.13), kind=kOutput, calls=%fused_computation.5 | convolution fusion | flops 41975808 | bytes 557056 | tf_op jit(solution)/shard_map/dot_general | solution.py:283
  1.4 1.3 %convolution_convert_fusion.2 = bf16[128,256]{1,0:T(8,128)(2,1)S(1)} fusion(bf16[128,640]{1,0:T(8,128)(2,1)} %param.11, bf16[640,256]{1,0:T(8,128)(2,1)} %param.14), kind=kOutput, calls=%fused_computation.4 | convolution fusion | flops 41975808 | bytes 557056 | tf_op jit(solution)/shard_map/dot_general | solution.py:284
  2.7 0.0 copy-done
  2.7 0.0 copy-start.4
  2.7 0.0 copy-start.2
  2.7 1.5 %convolution_convert_fusion = bf16[128,2048]{1,0:T(8,128)(2,1)S(1)} fusion(bf16[128,640]{1,0:T(8,128)(2,1)} %param.11, bf16[640,2048]{1,0:T(8,128)(2,1)S(1)} %copy-done), kind=kOutput, calls=%fused_computation | convolution fusion | flops 335806464 | bytes 3309568 | tf_op jit(solution)/shard_map/dot_general | solution.py:282
  4.2 0.0 copy-start.1
  4.3 0.0 copy-start.3
  4.3 0.9 pad_maximum_fusion
  5.2 5.2 %all-to-all-start = ((bf16[8,16,2560]{2,1,0:T(8,128)(2,1)}), bf16[8,16,2560]{2,1,0:T(8,128)(2,1)S(1)}, u32[]{:S(2)}, u32[]{:S(2)}) async-start(bf16[8,16,2560]{2,1,0:T(8,128)(2,1)} %pad_maximum_fusion), calls=%async_computation | async-start | bytes 1310720 | tf_op jit(solution)/shard_map/all_to_all | solution.py:251
  10.4 0.5 iota_add_fusion
  10.9 0.2 convert_reduce_fusion.1
  11.1 0.1 copy.66
  11.2 0.1 constant_dynamic-slice_fusion
  11.2 0.1 reshape.231
  11.3 0.1 dynamic-slice_convert_fusion
  11.4 0.1 copy.70
  11.5 0.7 select_reduce_fusion.order
  12.2 0.1 and_or_fusion
  12.3 0.1 multiply_cosine_fusion
  12.4 9.1 %all-to-all-done = bf16[8,16,2560]{2,1,0:T(8,128)(2,1)S(1)} async-done(((bf16[8,16,2560]{2,1,0:T(8,128)(2,1)}), bf16[8,16,2560]{2,1,0:T(8,128)(2,1)S(1)}, u32[]{:S(2)}, u32[]{:S(2)}) %all-to-all-start) | async-done | bytes 655392 | tf_op jit(solution)/shard_map/all_to_all | solution.py:251
  21.5 0.1 convert_reduce_fusion
  21.7 0.1 multiply_reduce_fusion.1
  21.8 0.1 multiply_reduce_fusion.2
  21.9 0.1 multiply_multiply_fusion
  22.0 0.1 multiply_multiply_fusion.1
  22.1 0.1 multiply_subtract_fusion
  22.2 0.1 subtract_convert_fusion
  22.3 0.1 maximum_convert_fusion
  22.4 9.9 %all_gather.6.q_ref = bf16[32,64,128]{2,1,0:T(8,128)(2,1)} all-gather(bf16[4,64,128]{2,1,0:T(8,128)(2,1)S(1)} %bitcast.50), channel_id=1, replica_groups=mesh['kv'=8,'head'=4] {'kv'}, dimensions={0}, use_global_device_ids=true | all-gather | bytes 589824 | tf_op jit(solution)/shard_map/all_gather | solution.py:294
  32.4 18.3 %shard_map.109 = bf16[32,80,128]{2,1,0:T(8,128)(2,1)} custom-call(s32[32]{0:T(128)} %select_reduce_fusion.order, s32[32]{0:T(128)} %get-tuple-element.10.live, bf16[32,64,128]{2,1,0:T(8,128)(2,1)} %all_gather.6.q_ref, bf16[32,2048,128]{2,1,0:T(8,128)(2,1)} %bitcast.44, bf16[32,2048,128]{2,1,0:T(8,128)(2,1)} %bitcast.45), custom_call_target="tpu_custom_call" | custom-call | tf_op jit(solution)/shard_map/pallas_call | solution.py:229
  50.6 3.6 %all-to-all-start.1 = ((bf16[8,4,80,128]{3,2,1,0:T(8,128)(2,1)}), bf16[8,4,80,128]{3,2,1,0:T(8,128)(2,1)S(1)}, u32[]{:S(2)}, u32[]{:S(2)}) async-start(bf16[8,4,80,128]{3,2,1,0:T(8,128)(2,1)} %bitcast.46), calls=%async_computation.1 | async-start | bytes 1310720 | tf_op jit(solution)/shard_map/all_to_all | solution.py:304
  54.2 0.1 pad_maximum_fusion.1
  54.3 0.4 fusion.18
  54.7 0.1 fusion.3
  54.9 0.1 reshape.239
  55.0 0.1 reshape.236
  55.1 0.3 convolution_bitcast_fusion
  55.4 9.9 %all-to-all-done.1 = bf16[8,4,80,128]{3,2,1,0:T(8,128)(2,1)S(1)} async-done(((bf16[8,4,80,128]{3,2,1,0:T(8,128)(2,1)}), bf16[8,4,80,128]{3,2,1,0:T(8,128)(2,1)S(1)}, u32[]{:S(2)}, u32[]{:S(2)}) %all-to-all-start.1) | async-done | bytes 655392 | tf_op jit(solution)/shard_map/all_to_all | solution.py:304
  65.3 0.1 fusion.17
  65.5 0.3 multiply_reduce_fusion
  65.9 0.1 div.35
  66.0 0.1 mul.218
  66.2 8.9 %all_gather.7 = bf16[128,2048]{1,0:T(8,128)(2,1)S(1)} all-gather(bf16[16,2048]{1,0:T(8,128)(2,1)S(1)} %divide_convert_fusion), channel_id=1, replica_groups=mesh['kv'=8,'head'=4] {'kv'}, dimensions={0}, use_global_device_ids=true | all-gather | bytes 589824 | tf_op jit(solution)/shard_map/all_gather | solution.py:344
  75.1 2.3 %convolution_convert_fusion.1 = bf16[128,640]{1,0:T(8,128)(2,1)S(1)} fusion(bf16[128,2048]{1,0:T(8,128)(2,1)S(1)} %all_gather.7, bf16[2048,640]{1,0:T(8,128)(2,1)} %param.21), kind=kOutput, calls=%fused_computation.2 | convolution fusion | flops 335626240 | bytes 3309568 | tf_op jit(solution)/shard_map/dot_general | solution.py:345
  77.4 11.9 %all_to_all.15 = bf16[4,32,640]{2,1,0:T(8,128)(2,1)S(1)} all-to-all(bf16[4,32,640]{2,1,0:T(8,128)(2,1)S(1)} %bitcast.49), channel_id=1, replica_groups=mesh['kv'=8,'head'=4] {'head'}, dimensions={0} | all-to-all | bytes 327680 | tf_op jit(solution)/shard_map/all_to_all | solution.py:251
  89.3 0.6 reduce_sum.95
  (27 shorter events, 0.4 us)
Async XLA Ops:
  0.0 2.7 %copy-start = (bf16[640,2048]{1,0:T(8,128)(2,1)S(1)}, bf16[640,2048]{1,0:T(8,128)(2,1)}, u32[]{:S(2)}) copy-start(bf16[640,2048]{1,0:T(8,128)(2,1)} %param.12) | copy-start | bytes 7864324
  2.7 7.6 %copy-start.4 = (s32[32]{0:T(128)S(1)}, s32[32]{0:T(128)}, u32[]{:S(2)}) copy-start(s32[32]{0:T(128)} %param.19) | copy-start | bytes 388
  2.7 8.3 %copy-start.2 = (s32[32,4]{0,1:T(4,128)S(1)}, s32[32,4]{0,1:T(4,128)}, u32[]{:S(2)}) copy-start(s32[32,4]{0,1:T(4,128)} %param.20) | copy-start | bytes 1540
  4.2 17.7 %copy-start.1 = (f32[16,128]{1,0:T(8,128)S(1)}, f32[16,128]{1,0:T(8,128)}, u32[]{:S(2)}) copy-start(f32[16,128]{1,0:T(8,128)} %param.15) | copy-start | bytes 24580
  4.3 17.8 %copy-start.3 = (f32[2,128]{1,0:T(2,128)S(1)}, f32[2,128]{1,0:T(2,128)}, u32[]{:S(2)}) copy-start(f32[2,128]{1,0:T(2,128)} %param.16) | copy-start | bytes 3076
  5.2 16.3 %all-to-all-start = ((bf16[8,16,2560]{2,1,0:T(8,128)(2,1)}), bf16[8,16,2560]{2,1,0:T(8,128)(2,1)S(1)}, u32[]{:S(2)}, u32[]{:S(2)}) async-start(bf16[8,16,2560]{2,1,0:T(8,128)(2,1)} %pad_maximum_fusion), calls=%async_computation | async-start | bytes 1310720 | tf_op jit(solution)/shard_map/all_to_all | solution.py:251
  50.6 14.6 %all-to-all-start.1 = ((bf16[8,4,80,128]{3,2,1,0:T(8,128)(2,1)}), bf16[8,4,80,128]{3,2,1,0:T(8,128)(2,1)S(1)}, u32[]{:S(2)}, u32[]{:S(2)}) async-start(bf16[8,4,80,128]{3,2,1,0:T(8,128)(2,1)} %bitcast.46), calls=%async_computation.1 | async-start | bytes 1310720 | tf_op jit(solution)/shard_map/all_to_all | solution.py:304

commit v7 on v6

--- a/solution.py
+++ b/solution.py
@@ -164,19 +164,29 @@
         ]
 
         def finish(results):
+            per_row = lanes // rows
+            stat_count = 5
+            stat_rows = (stat_count + per_row - 1) // per_row
+            lane = lax.broadcasted_iota(jnp.int32, (rows, lanes), 1)
+            blocks = [jnp.zeros((rows, lanes), jnp.float32) for _ in range(per_row)]
             for member, (m, l, acc) in enumerate(results):
                 alive = counts[member] > 0
                 m = jnp.where(alive, m, NEG)
                 l = jnp.where(alive, l, 0.0)
                 acc = jnp.where(alive, acc / jnp.where(alive, l, 1.0), 0.0)
                 out_ref[members[member], :rows, :] = acc.astype(out_ref.dtype)
-                stat_rows = [jnp.zeros((1, lanes), jnp.float32)] * (out_ref.shape[1] - rows)
-                for at, piece_group in enumerate(stat_groups(split_pieces(m, 3) + split_pieces(l, 2), lanes // rows)):
-                    pieces = [jnp.broadcast_to(v, (rows, lanes)) for v in piece_group]
-                    if lanes > rows * len(piece_group):
-                        pieces.append(jnp.zeros((lanes - rows * len(piece_group), lanes), jnp.float32))
-                    stat_rows[at] = jnp.transpose(jnp.concatenate(pieces, axis=0))[:1, :]
-                out_ref[members[member], rows:, :] = jnp.concatenate(stat_rows, axis=0).astype(out_ref.dtype)
+                vectors = split_pieces(m, 3) + split_pieces(l, 2)
+                for k, vector in enumerate(vectors):
+                    blocks[k % per_row] = jnp.where(
+                        lane == member * stat_rows + k // per_row, vector, blocks[k % per_row]
+                    )
+            if lanes > rows * per_row:
+                blocks.append(jnp.zeros((lanes - rows * per_row, lanes), jnp.float32))
+            flipped = jnp.transpose(jnp.concatenate(blocks, axis=0))
+            pad = jnp.zeros((out_ref.shape[1] - rows - stat_rows, lanes), jnp.float32)
+            for member in range(len(results)):
+                mine = flipped[member * stat_rows:(member + 1) * stat_rows, :]
+                out_ref[members[member], rows:, :] = jnp.concatenate([mine, pad], axis=0).astype(out_ref.dtype)
 
         @pl.when(top == 0)
         def _():
@@ -243,6 +253,49 @@
             pltpu.SemaphoreType.DMA((2, group, 2, flat_len // (sub * kv_local))),
         ],
     )(order, live, q_blocks, keys, values)
+
+
+def project_kernel(tokens_ref, q_ref, k_ref, v_ref, out_ref):
+    q_width = q_ref.shape[1]
+    k_width = k_ref.shape[1]
+    tokens = tokens_ref[...]
+    out_ref[:, :q_width] = jnp.dot(tokens, q_ref[...], preferred_element_type=jnp.float32).astype(out_ref.dtype)
+    out_ref[:, q_width:q_width + k_width] = jnp.dot(
+        tokens, k_ref[...], preferred_element_type=jnp.float32
+    ).astype(out_ref.dtype)
+    out_ref[:, q_width + k_width:] = jnp.dot(
+        tokens, v_ref[...], preferred_element_type=jnp.float32
+    ).astype(out_ref.dtype)
+
+
+def project(tokens, q_weight, key_matrix, value_matrix):
+    rows = tokens.shape[0]
+    width = q_weight.shape[1] + key_matrix.shape[1] + value_matrix.shape[1]
+    vmem = pltpu.MemorySpace.VMEM if hasattr(pltpu, "MemorySpace") else pltpu.TPUMemorySpace.VMEM
+    return pl.pallas_call(
+        project_kernel,
+        in_specs=[pl.BlockSpec(memory_space=vmem)] * 4,
+        out_specs=pl.BlockSpec(memory_space=vmem),
+        out_shape=jax.ShapeDtypeStruct((rows, width), jnp.bfloat16),
+    )(tokens, q_weight, key_matrix, value_matrix)
+
+
+def halving_sum(part, axis):
+    size = lax.axis_size(axis)
+    index = lax.axis_index(axis)
+    steps = log2_exact(size)
+    current = part
+    for step in reversed(range(steps)):
+        bit = 1 << step
+        keep = (index >> step) & 1
+        halves = current.reshape((2, current.shape[0] // 2) + current.shape[1:])
+        mine = lax.dynamic_index_in_dim(halves, keep, 0, False)
+        other = lax.dynamic_index_in_dim(halves, 1 - keep, 0, False)
+        if step == steps - 1:
+            other = other.astype(jnp.bfloat16)
+        received = lax.ppermute(other, axis, [(i, i ^ bit) for i in range(size)])
+        current = mine.astype(jnp.float32) + received.astype(jnp.float32)
+    return current
 
 
 def sum_over(part, axis):
@@ -277,15 +330,7 @@
     q_width = heads_local * head_dim
     k_width = kv_local * head_dim
 
-    proj = jnp.concatenate(
-        [
-            jnp.dot(tokens, q_weight, preferred_element_type=jnp.float32),
-            jnp.dot(tokens, key_matrix, preferred_element_type=jnp.float32),
-            jnp.dot(tokens, value_matrix, preferred_element_type=jnp.float32),
-        ],
-        axis=1,
-    )
-    proj_own = sum_over(proj.astype(jnp.bfloat16), "kv")
+    proj_own = sum_over(project(tokens, q_weight, key_matrix, value_matrix), "kv")
     pos_own = lax.dynamic_slice_in_dim(positions.reshape(rows), row0, own_rows)
     q_own = norm_rotate(proj_own[:, :q_width], q_gain, pos_own)
     k_own = norm_rotate(proj_own[:, q_width:q_width + k_width], key_norm_scale, pos_own)
@@ -343,7 +388,7 @@
     attended = (acc / total[..., None]).astype(jnp.bfloat16).reshape(own_rows, q_width)
     attended = lax.all_gather(attended, "kv", axis=0, tiled=True)
     partial_out = jnp.dot(attended, o_weight, preferred_element_type=jnp.float32)
-    return sum_over(partial_out.astype(jnp.bfloat16), "head").astype(jnp.bfloat16)
+    return halving_sum(partial_out, "head").astype(jnp.bfloat16)
 
 
 def solution(mesh):

time: 90.5 us -> 88 us (0.972)
  blocking collectives: 30.7 us -> 18.8 us
  waiting for transfers between devices: 19 us -> 27.5 us
  matrix products: 7.22 us -> 1.29 us
  Pallas kernels: 18.3 us -> 22.9 us
  starting transfers between devices: 8.72 us -> 12.3 us
    all_to_all x1 -> x0, blocking collectives: 11.9 us -> none  [sum_over(): lax.all_to_all(split, axis, 0, 0).astype(jnp.float32)]
    ppermute x0 -> x2, waiting for transfers between devices: none -> 8.51 us  [halving_sum(): received = lax.ppermute(other, axis, [(i, i ^ bit) for i in range(size)])]
    dot_general x3 -> x0, matrix products: 4.19 us -> none  [the longest x1 1.5 us: on_device(): jnp.dot(tokens, q_weight, preferred_element_type=jnp.float32)]
    pallas_call x0 -> x1, Pallas kernels: none -> 3.57 us  [project(): pl.pallas_call(project_kernel, in_specs=[pl.BlockSpec(memory_space=vmem)]...]
    ppermute x0 -> x2, starting transfers between devices: none -> 3.42 us  [halving_sum(): received = lax.ppermute(other, axis, [(i, i ^ bit) for i in range(size)])]
    dot_general x1, matrix products: 2.32 us -> 0.58 us  [on_device(): jnp.dot(attended, o_weight, preferred_element_type=jnp.float32)]
    pallas_call x1, Pallas kernels: 18.3 us -> 19.3 us  [cache_attention(): pl.pallas_call(kernel, in_specs=[pl.BlockSpec(memory_space=pltpu.SMEM), p...]
  transfers between devices with their start and end apart: 2 -> 4, of which waited for: 2 -> 4; matrix products, arithmetic and copies ran while one was open for 4% -> 4% of each run, Pallas kernels for 0% -> 0%
where the time goes in v7:
time: 88 us; the launch traced here: 87.9 us
  waiting for transfers between devices  27.5 us (31%)
  Pallas kernels  22.9 us (26%)
  blocking collectives  18.8 us (21%)
  starting transfers between devices  12.3 us (14%)
  other arithmetic  3.88 us (4%)
  matrix products  1.29 us (1%)
  local copies, waits for them, and re-layouts  0.99 us (1%)
    pallas_call x1, Pallas kernels, cache_attention(): pl.pallas_call(kernel, in_specs=[pl.BlockSpec(memory_space=pltpu.SMEM), p...  19.3 us
    all_gather x1, blocking collectives, on_device(): lax.all_gather(q_own.reshape(own_reqs, rows_r, head_dim), 'kv', axis=0, t...  9.93 us
    all_to_all x1, waiting for transfers between devices, on_device(): lax.all_to_all(partial.reshape((kv_size, own_reqs) + partial.shape[1:]),...  9.88 us
    all_to_all x1, waiting for transfers between devices, sum_over(): lax.all_to_all(split, axis, 0, 0).astype(jnp.float32)  9.09 us
    all_gather x1, blocking collectives, on_device(): attended = lax.all_gather(attended, 'kv', axis=0, tiled=True)  8.9 us
    ppermute x2, waiting for transfers between devices, halving_sum(): received = lax.ppermute(other, axis, [(i, i ^ bit) for i in range(size)])  8.51 us
    all_to_all x1, starting transfers between devices, sum_over(): lax.all_to_all(split, axis, 0, 0).astype(jnp.float32)  5.31 us
    pallas_call x1, Pallas kernels, project(): pl.pallas_call(project_kernel, in_specs=[pl.BlockSpec(memory_space=vmem)]...  3.57 us
  transfers between devices with their start and end apart: 4, of which 4 were waited for; matrix products, arithmetic and copies ran while one was open for 4% of the time, Pallas kernels for 0%

profile of v7, /device:TPU:0, one launch (start us, length us, event | category | flops | bytes accessed | tf_op | source)
XLA Modules:
  0.0 87.9 jit_solution(16304450733659379568)
XLA Ops:
  0.0 0.0 copy-start
  0.0 3.6 %shard_map.109 = bf16[128,2560]{1,0:T(8,128)(2,1)} custom-call(bf16[128,640]{1,0:T(8,128)(2,1)} %tokens_ref.1, bf16[640,2048]{1,0:T(8,128)(2,1)} %q_ref.1, bf16[640,256]{1,0:T(8,128)(2,1)} %k_ref.1, bf16[640,256]{1,0:T(8,128)(2,1)} %v_ref.1), custom_call_target="tpu_custom_call" | custom-call | tf_op jit(solution)/shard_map/pallas_call | solution.py:275
  3.6 5.3 %all-to-all-start = ((bf16[8,16,2560]{2,1,0:T(8,128)(2,1)}), bf16[8,16,2560]{2,1,0:T(8,128)(2,1)S(1)}, u32[]{:S(2)}, u32[]{:S(2)}) async-start(bf16[8,16,2560]{2,1,0:T(8,128)(2,1)} %bitcast.49), calls=%async_computation | async-start | bytes 1310720 | tf_op jit(solution)/shard_map/all_to_all | solution.py:304
  8.9 0.0 copy-done.4
  8.9 0.5 iota_add_fusion
  9.5 0.2 convert_reduce_fusion.1
  9.6 0.0 copy-done.2
  9.6 0.1 copy.66
  9.7 0.1 constant_dynamic-slice_fusion
  9.8 0.1 reshape.232
  9.9 0.1 dynamic-slice_convert_fusion.1
  10.0 0.1 copy.70
  10.1 0.7 select_reduce_fusion.order
  10.8 0.1 and_or_fusion
  10.8 0.1 multiply_cosine_fusion
  11.0 9.1 %all-to-all-done = bf16[8,16,2560]{2,1,0:T(8,128)(2,1)S(1)} async-done(((bf16[8,16,2560]{2,1,0:T(8,128)(2,1)}), bf16[8,16,2560]{2,1,0:T(8,128)(2,1)S(1)}, u32[]{:S(2)}, u32[]{:S(2)}) %all-to-all-start) | async-done | bytes 655392 | tf_op jit(solution)/shard_map/all_to_all | solution.py:304
  20.1 0.1 convert_reduce_fusion
  20.2 0.1 multiply_reduce_fusion.1
  20.4 0.1 multiply_reduce_fusion.2
  20.5 0.0 copy-done.1
  20.5 0.1 multiply_multiply_fusion
  20.6 0.0 copy-done.3
  20.6 0.1 multiply_multiply_fusion.1
  20.7 0.1 multiply_subtract_fusion
  20.8 0.1 subtract_convert_fusion
  20.9 0.1 maximum_convert_fusion
  21.0 9.9 %all_gather.6.q_ref = bf16[32,64,128]{2,1,0:T(8,128)(2,1)} all-gather(bf16[4,64,128]{2,1,0:T(8,128)(2,1)S(1)} %bitcast.56), channel_id=1, replica_groups=mesh['kv'=8,'head'=4] {'kv'}, dimensions={0}, use_global_device_ids=true | all-gather | bytes 589824 | tf_op jit(solution)/shard_map/all_gather | solution.py:339
  30.9 19.3 %shard_map.110 = bf16[32,80,128]{2,1,0:T(8,128)(2,1)} custom-call(s32[32]{0:T(128)} %select_reduce_fusion.order, s32[32]{0:T(128)} %get-tuple-element.10.live, bf16[32,64,128]{2,1,0:T(8,128)(2,1)} %all_gather.6.q_ref, bf16[32,2048,128]{2,1,0:T(8,128)(2,1)} %bitcast.47, bf16[32,2048,128]{2,1,0:T(8,128)(2,1)} %bitcast.48), custom_call_target="tpu_custom_call" | custom-call | tf_op jit(solution)/shard_map/pallas_call | solution.py:239
  50.2 3.6 %all-to-all-start.1 = ((bf16[8,4,80,128]{3,2,1,0:T(8,128)(2,1)}), bf16[8,4,80,128]{3,2,1,0:T(8,128)(2,1)S(1)}, u32[]{:S(2)}, u32[]{:S(2)}) async-start(bf16[8,4,80,128]{3,2,1,0:T(8,128)(2,1)} %bitcast.50), calls=%async_computation.1 | async-start | bytes 1310720 | tf_op jit(solution)/shard_map/all_to_all | solution.py:349
  53.8 0.1 pad_maximum_fusion
  53.9 0.4 fusion.20
  54.3 0.1 fusion.5
  54.5 0.1 reshape.240
  54.5 0.1 reshape.237
  54.6 0.3 convolution_bitcast_fusion
  55.0 9.9 %all-to-all-done.1 = bf16[8,4,80,128]{3,2,1,0:T(8,128)(2,1)S(1)} async-done(((bf16[8,4,80,128]{3,2,1,0:T(8,128)(2,1)}), bf16[8,4,80,128]{3,2,1,0:T(8,128)(2,1)S(1)}, u32[]{:S(2)}, u32[]{:S(2)}) %all-to-all-start.1) | async-done | bytes 655392 | tf_op jit(solution)/shard_map/all_to_all | solution.py:349
  64.9 0.1 fusion.19
  65.1 0.3 multiply_reduce_fusion
  65.5 0.1 div.35
  65.6 0.1 mul.218
  65.8 8.9 %all_gather.7 = bf16[128,2048]{1,0:T(8,128)(2,1)S(1)} all-gather(bf16[16,2048]{1,0:T(8,128)(2,1)S(1)} %divide_convert_fusion), channel_id=1, replica_groups=mesh['kv'=8,'head'=4] {'kv'}, dimensions={0}, use_global_device_ids=true | all-gather | bytes 589824 | tf_op jit(solution)/shard_map/all_gather | solution.py:389
  74.7 0.0 copy-done
  74.7 0.6 fusion.21
  75.3 2.7 %collective-permute-start = (bf16[64,640]{1,0:T(8,128)(2,1)S(1)}, bf16[64,640]{1,0:T(8,128)(2,1)S(1)}, u32[]{:S(2)}, u32[]{:S(2)}) collective-permute-start(bf16[64,640]{1,0:T(8,128)(2,1)S(1)} %fusion.2), channel_id=1, source_target_pairs={{0,2},{1,3},{2,0},{3,1},{4,6},{5,7},{6,4},{7,5},{8,10},{9,11},{10,... | collective-permute-start | bytes 245768 | tf_op jit(solution)/shard_map/ppermute | solution.py:296
  78.0 4.8 %collective-permute-done = bf16[64,640]{1,0:T(8,128)(2,1)S(1)} collective-permute-done((bf16[64,640]{1,0:T(8,128)(2,1)S(1)}, bf16[64,640]{1,0:T(8,128)(2,1)S(1)}, u32[]{:S(2)}, u32[]{:S(2)}) %collective-permute-start) | collective-permute-done | bytes 81952 | tf_op jit(solution)/shard_map/ppermute | solution.py:296
  82.8 0.8 collective-permute-start.1
  83.5 3.7 %collective-permute-done.1 = f32[32,640]{1,0:T(8,128)S(1)} collective-permute-done((f32[32,640]{1,0:T(8,128)S(1)}, f32[32,640]{1,0:T(8,128)S(1)}, u32[]{:S(2)}, u32[]{:S(2)}) %collective-permute-start.1) | collective-permute-done | bytes 81952 | tf_op jit(solution)/shard_map/ppermute | solution.py:296
  87.3 0.6 fusion.3
  (30 shorter events, 0.4 us)
Async XLA Ops:
  0.0 74.7 %copy-start = (bf16[2048,640]{1,0:T(8,128)(2,1)S(1)}, bf16[2048,640]{1,0:T(8,128)(2,1)}, u32[]{:S(2)}) copy-start(bf16[2048,640]{1,0:T(8,128)(2,1)} %param.21) | copy-start | bytes 7864324
  0.0 8.9 %copy-start.4 = (s32[32]{0:T(128)S(1)}, s32[32]{0:T(128)}, u32[]{:S(2)}) copy-start(s32[32]{0:T(128)} %param.19) | copy-start | bytes 388
  0.0 9.6 %copy-start.2 = (s32[32,4]{0,1:T(4,128)S(1)}, s32[32,4]{0,1:T(4,128)}, u32[]{:S(2)}) copy-start(s32[32,4]{0,1:T(4,128)} %param.20) | copy-start | bytes 1540
  0.0 20.5 %copy-start.1 = (f32[16,128]{1,0:T(8,128)S(1)}, f32[16,128]{1,0:T(8,128)}, u32[]{:S(2)}) copy-start(f32[16,128]{1,0:T(8,128)} %param.15) | copy-start | bytes 24580
  3.6 17.0 %copy-start.3 = (f32[2,128]{1,0:T(2,128)S(1)}, f32[2,128]{1,0:T(2,128)}, u32[]{:S(2)}) copy-start(f32[2,128]{1,0:T(2,128)} %param.16) | copy-start | bytes 3076
  3.6 16.5 %all-to-all-start = ((bf16[8,16,2560]{2,1,0:T(8,128)(2,1)}), bf16[8,16,2560]{2,1,0:T(8,128)(2,1)S(1)}, u32[]{:S(2)}, u32[]{:S(2)}) async-start(bf16[8,16,2560]{2,1,0:T(8,128)(2,1)} %bitcast.49), calls=%async_computation | async-start | bytes 1310720 | tf_op jit(solution)/shard_map/all_to_all | solution.py:304
  50.2 14.6 %all-to-all-start.1 = ((bf16[8,4,80,128]{3,2,1,0:T(8,128)(2,1)}), bf16[8,4,80,128]{3,2,1,0:T(8,128)(2,1)S(1)}, u32[]{:S(2)}, u32[]{:S(2)}) async-start(bf16[8,4,80,128]{3,2,1,0:T(8,128)(2,1)} %bitcast.50), calls=%async_computation.1 | async-start | bytes 1310720 | tf_op jit(solution)/shard_map/all_to_all | solution.py:349
  75.3 7.4 %collective-permute-start = (bf16[64,640]{1,0:T(8,128)(2,1)S(1)}, bf16[64,640]{1,0:T(8,128)(2,1)S(1)}, u32[]{:S(2)}, u32[]{:S(2)}) collective-permute-start(bf16[64,640]{1,0:T(8,128)(2,1)S(1)} %fusion.2), channel_id=1, source_target_pairs={{0,2},{1,3},{2,0},{3,1},{4,6},{5,7},{6,4},{7,5},{8,10},{9,11},{10,... | collective-permute-start | bytes 245768 | tf_op jit(solution)/shard_map/ppermute | solution.py:296
  82.8 4.5 %collective-permute-start.1 = (f32[32,640]{1,0:T(8,128)S(1)}, f32[32,640]{1,0:T(8,128)S(1)}, u32[]{:S(2)}, u32[]{:S(2)}) collective-permute-start(f32[32,640]{1,0:T(8,128)S(1)} %dynamic-slice_bitcast_fusion), channel_id=1, source_target_pairs={{0,1},{1,0},{2,3},{3,2},{4,5},{5,4},{6,7},{7,6},{8,9},{9,8},{10,11... | collective-permute-start | bytes 245768 | tf_op jit(solution)/shard_map/ppermute | solution.py:296
